TPU v7x, 128 devices: a whole 4x4x4 slice. The times are simulated.
128 devices in a mesh: seq: 16 (over x, y), tensor: 8 (over z, core).
Axes of the slice: x: 4, y: 4, z: 4, core: 2. Of those that a mesh axis runs over, the one named last changes fastest.
Arguments:
- tokens: bfloat16 [12288, 2048], P('seq'), may hold values from -6 to 6
- norm_gain: float32 [2048], replicated, may hold values from 0.1 to 1.9
- query_weight: bfloat16 [2048, 2048], P(None, 'tensor'), may hold values from -0.125 to 0.125
- key_value_matrix: bfloat16 [2048, 4, 128], replicated, may hold values from -0.125 to 0.125
- out_weight: bfloat16 [2048, 2048], replicated, may hold values from -0.125 to 0.125
- cache_pages: bfloat16 [1024, 4, 128, 128], P('seq'), may hold values from -180 to 180, as said below
- page_table: int32 [16, 64], replicated, may hold values from 0 to 1023, as said below
- request_lengths: int32 [80], replicated, may hold values from 1 to 764, as said below
- request_groups: int32 [80], replicated, may hold values from 0 to 15
Outputs:
- projected: bfloat16 [12288, 2048], P('seq', 'tensor')
Inputs may be any that keep to these rules, and one draw needn't show every extreme that they name: `page_table`: every page id appears once. Of the last 16 entries of each row, exactly 1 lie in each block of 64 consecutive ids, the pages held by one seq device. `request_lengths`: the lengths of the 5 requests of one seq device sum to at most 768, and to exactly 768 on at least one device. `cache_pages`: keys in the first 64 entries of the last dimension, values in the rest.
All inputs are finite; a program needn't handle non-finite values.
Results may differ from a plain program's by a relative error of at most 0.012.
The roundings to bfloat16 on the way count: a program that leaves them out, or rounds other values in their place, can miss the bound.
Values may be sent and summed in bfloat16 or wider, within the bound.
No kernel may reach another device: no remote copies, remote signals or barrier semaphores. Data moves between devices by JAX's collectives and lax.ppermute only.
A program may use at most 128 MiB of HBM per device.

v0:
```python
import math

import jax
import jax.numpy as jnp
from jax import lax
from jax.sharding import PartitionSpec as P

QUERY_HEADS = 32
KEY_VALUE_HEADS = 4
HEAD_SIZE = 64
WINDOW_LENGTH = 2048
DEVICE_REQUESTS = 5
PPG = 64
WP = 16


MASKED_SCORE = -1e30


def normalize(tokens, norm_gain):
    widened = tokens.astype(jnp.float32)
    factor = lax.rsqrt(jnp.mean(widened * widened, axis=-1, keepdims=True) + 1e-05)
    return (widened * factor * norm_gain).astype(jnp.bfloat16)


def row_layout(lengths, row_total_count):
    request_ends = jnp.cumsum(lengths)
    starts = request_ends - lengths
    slot_ids = lax.iota(jnp.int32, row_total_count)
    row_request = jnp.sum((slot_ids[:, None] >= request_ends[None, :]).astype(jnp.int32), axis=1)
    row_live = slot_ids < request_ends[-1]
    choose = row_request[:, None] == lax.iota(jnp.int32, lengths.shape[0])[None, :]
    begins = jnp.sum(jnp.where(choose, starts[None, :], 0), axis=1)
    return (row_request, row_live, slot_ids - begins)


def lookup_rows(table, wanted):
    table_rows = table.shape[0]
    matches = wanted[:, None] == lax.iota(jnp.int32, table_rows)[None, :]
    return jnp.sum(jnp.where(matches[:, :, None], table[None, :, :], 0), axis=1)


def body(
    tokens,
    norm_gain,
    query_weight,
    key_value_matrix,
    out_weight,
    cache_pages,
    page_table,
    request_lengths,
    request_groups,
):
    seq_count = lax.axis_size("seq")
    seq_index = lax.axis_index("seq")
    tensor_rank_index = lax.axis_index("tensor")
    row_count = tokens.shape[0]
    resident_heads = query_weight.shape[1] // HEAD_SIZE
    key_value_head = tensor_rank_index * resident_heads // (QUERY_HEADS // KEY_VALUE_HEADS)
    group_count = page_table.shape[0]
    per_owner = WP // seq_count
    pages_here = cache_pages.shape[0]
    score_scale = HEAD_SIZE ** (-0.5)
    normed = normalize(tokens, norm_gain)
    query_rows = jnp.dot(normed, query_weight, preferred_element_type=jnp.float32).astype(
        jnp.bfloat16
    )
    query_rows = query_rows.reshape(row_count, resident_heads, HEAD_SIZE)
    head_weight = lax.dynamic_index_in_dim(key_value_matrix, key_value_head, 1, keepdims=False)
    new_token_rows = jnp.dot(normed, head_weight, preferred_element_type=jnp.float32).astype(
        jnp.bfloat16
    )
    lengths = lax.dynamic_slice_in_dim(
        request_lengths, seq_index * DEVICE_REQUESTS, DEVICE_REQUESTS
    )
    my_groups = lax.dynamic_slice_in_dim(
        request_groups, seq_index * DEVICE_REQUESTS, DEVICE_REQUESTS
    )
    row_request, row_live, row_position = row_layout(lengths, row_count)
    tail_ids = page_table[:, PPG - WP :]
    holder = tail_ids // pages_here
    local_slot = tail_ids % pages_here
    earlier = lax.iota(jnp.int32, WP)[:, None] > lax.iota(jnp.int32, WP)[None, :]
    same_owner = holder[:, :, None] == holder[:, None, :]
    tail_rank = jnp.sum((same_owner & earlier[None, :, :]).astype(jnp.int32), axis=2)
    tail_hit = (holder == seq_index)[:, :, None] & (
        tail_rank[:, :, None] == lax.iota(jnp.int32, per_owner)[None, None, :]
    )
    tail_pick = jnp.sum(jnp.where(tail_hit, local_slot[:, :, None], 0), axis=1)
    head_pages = lax.dynamic_index_in_dim(cache_pages, key_value_head, 1, keepdims=False)
    my_holder = lookup_rows(holder, my_groups)
    my_rank = lookup_rows(tail_rank, my_groups)
    outgoing = head_pages[tail_pick.reshape(-1)]
    gathered = lax.all_gather(outgoing, "seq", axis=0, tiled=True)
    where_from = my_holder * (group_count * per_owner) + my_groups[:, None] * per_owner + my_rank
    window_rows = gathered[where_from.reshape(-1)]
    window_rows = window_rows.reshape(DEVICE_REQUESTS, WINDOW_LENGTH, 2 * HEAD_SIZE)
    offsets = lax.iota(jnp.int32, WINDOW_LENGTH)
    column = lax.iota(jnp.int32, row_count)
    fresh_keys = new_token_rows[:, :HEAD_SIZE]
    fresh_values = new_token_rows[:, HEAD_SIZE:]
    block_size = math.gcd(row_count, 128)
    block_count = row_count // block_size

    def one_block(block_inputs):
        block_query, block_request, block_live, block_position, block_column = block_inputs
        first_request = jnp.min(block_request)
        last_request = jnp.minimum(jnp.max(block_request), DEVICE_REQUESTS - 1)

        def add_scores(request_slot, running):
            keys_here = lax.dynamic_index_in_dim(window_rows, request_slot, 0, keepdims=False)[
                :, :HEAD_SIZE
            ]
            scores_one = (
                jnp.einsum(
                    "rhd,md->hrm", block_query, keys_here, preferred_element_type=jnp.float32
                )
                * score_scale
            )
            return jnp.where((block_request == request_slot)[None, :, None], scores_one, running)

        prefix_scores = lax.fori_loop(
            first_request,
            last_request + 1,
            add_scores,
            jnp.zeros((resident_heads, block_size, WINDOW_LENGTH), jnp.float32),
        )
        suffix_scores = (
            jnp.einsum("rhd,cd->hrc", block_query, fresh_keys, preferred_element_type=jnp.float32)
            * score_scale
        )
        prefix_mask = block_live[:, None] & (offsets[None, :] >= block_position[:, None] + 1)
        suffix_mask = (
            (block_request[:, None] == row_request[None, :])
            & block_live[:, None]
            & (column[None, :] <= block_column[:, None])
            & (block_column[:, None] - column[None, :] < WINDOW_LENGTH)
        )
        row_top = jnp.maximum(
            jnp.max(jnp.where(prefix_mask[None], prefix_scores, MASKED_SCORE), axis=2),
            jnp.max(jnp.where(suffix_mask[None], suffix_scores, MASKED_SCORE), axis=2),
        )
        prefix_raw = jnp.where(prefix_mask[None], jnp.exp(prefix_scores - row_top[:, :, None]), 0.0)
        suffix_raw = jnp.where(suffix_mask[None], jnp.exp(suffix_scores - row_top[:, :, None]), 0.0)
        row_total = jnp.sum(prefix_raw, axis=2) + jnp.sum(suffix_raw, axis=2)
        prefix_weights = prefix_raw.astype(jnp.bfloat16)
        suffix_weights = suffix_raw.astype(jnp.bfloat16)
        weighted = jnp.einsum(
            "hrc,cd->rhd", suffix_weights, fresh_values, preferred_element_type=jnp.float32
        )

        def add_values(request_slot, running):
            values_here = lax.dynamic_index_in_dim(window_rows, request_slot, 0, keepdims=False)[
                :, HEAD_SIZE:
            ]
            chosen = jnp.where(
                (block_request == request_slot)[None, :, None],
                prefix_weights,
                jnp.zeros((), jnp.bfloat16),
            )
            return running + jnp.einsum(
                "hrm,md->rhd", chosen, values_here, preferred_element_type=jnp.float32
            )

        weighted = lax.fori_loop(first_request, last_request + 1, add_values, weighted)
        safe_total = jnp.where(block_live[None, :], row_total, 1.0)
        block_out = jnp.where(
            block_live[:, None, None], weighted / jnp.transpose(safe_total)[:, :, None], 0.0
        )
        return block_out.astype(jnp.bfloat16).reshape(block_size, resident_heads * HEAD_SIZE)

    block_inputs = (
        query_rows.reshape(block_count, block_size, resident_heads, HEAD_SIZE),
        row_request.reshape(block_count, block_size),
        row_live.reshape(block_count, block_size),
        row_position.reshape(block_count, block_size),
        column.reshape(block_count, block_size),
    )
    attended = lax.map(one_block, block_inputs).reshape(row_count, resident_heads * HEAD_SIZE)
    my_rows = lax.dynamic_slice_in_dim(
        out_weight, tensor_rank_index * resident_heads * HEAD_SIZE, resident_heads * HEAD_SIZE, 0
    )
    partial_terms = jnp.dot(attended, my_rows, preferred_element_type=jnp.float32)
    projected = lax.psum_scatter(partial_terms, "tensor", scatter_dimension=1, tiled=True)
    return projected.astype(jnp.bfloat16)


def solution(mesh):
    return jax.shard_map(
        body,
        mesh=mesh,
        in_specs=(
            P("seq", None),
            P(),
            P(None, "tensor"),
            P(),
            P(),
            P("seq", None, None, None),
            P(),
            P(),
            P(),
        ),
        out_specs=P("seq", "tensor"),
        check_vma=False,
    )
```

profile of v0, /device:TPU:1, one launch (start us, length us, event | category | flops | bytes accessed | tf_op | source)
XLA Modules:
  0.0 402.1 jit_solution(16666838401920987250)
XLA Ops:
  27.8 61.2 %all-gather.3.cloned.1.call-done = bf16[256,128,128]{2,1,0:T(8,128)(2,1)} async-done(((bf16[16,128,128]{2,1,0:T(8,128)(2,1)}), bf16[256,128,128]{2,1,0:T(8,128)(2,1)}) %all-gather.3.cloned.1.call-update) | async-done | bytes 8388624 | tf_op jit(solution)/shard_map/all_gather | solution.py:94
  89.0 6.0 %gather_fusion.1 = bf16[80,128,128]{2,1,0:T(8,128)(2,1)} fusion(bf16[256,128,128]{2,1,0:T(8,128)(2,1)} %all-gather.3.cloned.1.call-done, s32[1024]{0:T(1024)S(1)} %pad_clamp_fusion), kind=kCustom, calls=%fused_computation.1 | custom fusion | bytes 5243200 | tf_op jit(solution)/shard_map/gather | solution.py:96
  99.5 246.8 %while.38 = (s32[]{:T(128)}, bf16[6,128,256]{2,1,0:T(8,128)(2,1)S(1)}, pred[6,128]{1,0:T(8,128)(4,1)S(1)}, s32[6,128]{1,0:T(8,128)S(1)}, s32[768]{0:T(1024)S(1)}...) while((s32[]{:T(128)}, ...), condition=%wide.region_19.20_spmd.clone.clone, body=%wide.region_8.19_spmd.clone.clone.sunk | while | flops 383418496 | bytes 60202160 | solution.py:179
  103.8 12.1 %while.39 = (s32[]{:T(128)}, f32[4,128,2048]{1,2,0:T(8,128)}, s32[]{:T(128)}, s32[128]{0:T(128)S(1)}, bf16[5,2048,128]{1,2,0:T(8,128)(2,1)}, /*index=5*/bf16[128...) while((s32[]{:T(128)}, f32[4,128,2048]{1,2,0:T(8,128)}, s32[]{:T(128)}, s32[128]{0:T(128)S(1)}, ...), condition=%wide.region_12.12_spmd, body=%wide.region_11.11_spmd.sunk | while | flops 136315008 | bytes 9766151 | solution.py:122
  104.9 4.9 %bitcast_select_fusion.3 = f32[4,128,2048]{1,2,0:T(8,128)} fusion(f32[4,128,2048]{1,2,0:T(8,128)} %get-tuple-element.531, bf16[128,4,64]{0,2,1:T(8,128)(2,1)S(1)} %get-tuple-element.544, pred[128]{0:T(512)(128)(4,1)S(1)} %broadcast_compare_fusion.4, bf16[2048,128]{0,1:T(8,128)(2,1)S(1)} %dynamic-slice_bitcast_fusion.12), kind=kOutput, calls=%fused_computation.4.clone.1 | convolution fusion | flops 136314880 | bytes 8716800 | tf_op jit(solution)/shard_map/while/body/eval_jaxpr/while/body/rhd,md->hrm/dot_general | solution.py:115
  111.0 4.9 %bitcast_select_fusion.3 = f32[4,128,2048]{1,2,0:T(8,128)} fusion(f32[4,128,2048]{1,2,0:T(8,128)} %get-tuple-element.531, bf16[128,4,64]{0,2,1:T(8,128)(2,1)S(1)} %get-tuple-element.544, pred[128]{0:T(512)(128)(4,1)S(1)} %broadcast_compare_fusion.4, bf16[2048,128]{0,1:T(8,128)(2,1)S(1)} %dynamic-slice_bitcast_fusion.12), kind=kOutput, calls=%fused_computation.4.clone.1 | convolution fusion | flops 136314880 | bytes 8716800 | tf_op jit(solution)/shard_map/while/body/eval_jaxpr/while/body/rhd,md->hrm/dot_general | solution.py:115
  115.9 5.4 %copy.49 = f32[4,128,2048]{2,1,0:T(8,128)} copy(f32[4,128,2048]{1,2,0:T(8,128)} %get-tuple-element.503) | data formatting | bytes 8388608 | tf_op jit(solution)/shard_map/while/body/eval_jaxpr/while | solution.py:122
  128.6 16.5 %while.40 = (s32[]{:T(128)}, f32[128,4,64]{0,2,1:T(8,128)S(1)}, s32[]{:T(128)}, bf16[5,2048,128]{1,2,0:T(8,128)(2,1)}, s32[128]{0:T(128)S(1)}, /*index=5*/bf16[4...) while((s32[]{:T(128)}, f32[128,4,64]{0,2,1:T(8,128)S(1)}, s32[]{:T(128)}, ...), condition=%wide.region_16.16_spmd, body=%wide.region_15.15_spmd.sunk | while | flops 135299200 | bytes 3671303 | solution.py:165
  149.6 18.1 %while.39 = (s32[]{:T(128)}, f32[4,128,2048]{1,2,0:T(8,128)}, s32[]{:T(128)}, s32[128]{0:T(128)S(1)}, bf16[5,2048,128]{1,2,0:T(8,128)(2,1)}, /*index=5*/bf16[128...) while((s32[]{:T(128)}, f32[4,128,2048]{1,2,0:T(8,128)}, s32[]{:T(128)}, s32[128]{0:T(128)S(1)}, ...), condition=%wide.region_12.12_spmd, body=%wide.region_11.11_spmd.sunk | while | flops 136315008 | bytes 9766151 | solution.py:122
  150.7 4.9 %bitcast_select_fusion.3 = f32[4,128,2048]{1,2,0:T(8,128)} fusion(f32[4,128,2048]{1,2,0:T(8,128)} %get-tuple-element.531, bf16[128,4,64]{0,2,1:T(8,128)(2,1)S(1)} %get-tuple-element.544, pred[128]{0:T(512)(128)(4,1)S(1)} %broadcast_compare_fusion.4, bf16[2048,128]{0,1:T(8,128)(2,1)S(1)} %dynamic-slice_bitcast_fusion.12), kind=kOutput, calls=%fused_computation.4.clone.1 | convolution fusion | flops 136314880 | bytes 8716800 | tf_op jit(solution)/shard_map/while/body/eval_jaxpr/while/body/rhd,md->hrm/dot_general | solution.py:115
  156.7 4.9 %bitcast_select_fusion.3 = f32[4,128,2048]{1,2,0:T(8,128)} fusion(f32[4,128,2048]{1,2,0:T(8,128)} %get-tuple-element.531, bf16[128,4,64]{0,2,1:T(8,128)(2,1)S(1)} %get-tuple-element.544, pred[128]{0:T(512)(128)(4,1)S(1)} %broadcast_compare_fusion.4, bf16[2048,128]{0,1:T(8,128)(2,1)S(1)} %dynamic-slice_bitcast_fusion.12), kind=kOutput, calls=%fused_computation.4.clone.1 | convolution fusion | flops 136314880 | bytes 8716800 | tf_op jit(solution)/shard_map/while/body/eval_jaxpr/while/body/rhd,md->hrm/dot_general | solution.py:115
  162.8 4.9 %bitcast_select_fusion.3 = f32[4,128,2048]{1,2,0:T(8,128)} fusion(f32[4,128,2048]{1,2,0:T(8,128)} %get-tuple-element.531, bf16[128,4,64]{0,2,1:T(8,128)(2,1)S(1)} %get-tuple-element.544, pred[128]{0:T(512)(128)(4,1)S(1)} %broadcast_compare_fusion.4, bf16[2048,128]{0,1:T(8,128)(2,1)S(1)} %dynamic-slice_bitcast_fusion.12), kind=kOutput, calls=%fused_computation.4.clone.1 | convolution fusion | flops 136314880 | bytes 8716800 | tf_op jit(solution)/shard_map/while/body/eval_jaxpr/while/body/rhd,md->hrm/dot_general | solution.py:115
  167.7 5.4 %copy.49 = f32[4,128,2048]{2,1,0:T(8,128)} copy(f32[4,128,2048]{1,2,0:T(8,128)} %get-tuple-element.503) | data formatting | bytes 8388608 | tf_op jit(solution)/shard_map/while/body/eval_jaxpr/while | solution.py:122
  180.5 24.4 %while.40 = (s32[]{:T(128)}, f32[128,4,64]{0,2,1:T(8,128)S(1)}, s32[]{:T(128)}, bf16[5,2048,128]{1,2,0:T(8,128)(2,1)}, s32[128]{0:T(128)S(1)}, /*index=5*/bf16[4...) while((s32[]{:T(128)}, f32[128,4,64]{0,2,1:T(8,128)S(1)}, s32[]{:T(128)}, ...), condition=%wide.region_16.16_spmd, body=%wide.region_15.15_spmd.sunk | while | flops 135299200 | bytes 3671303 | solution.py:165
  209.4 6.0 %while.39 = (s32[]{:T(128)}, f32[4,128,2048]{1,2,0:T(8,128)}, s32[]{:T(128)}, s32[128]{0:T(128)S(1)}, bf16[5,2048,128]{1,2,0:T(8,128)(2,1)}, /*index=5*/bf16[128...) while((s32[]{:T(128)}, f32[4,128,2048]{1,2,0:T(8,128)}, s32[]{:T(128)}, s32[128]{0:T(128)S(1)}, ...), condition=%wide.region_12.12_spmd, body=%wide.region_11.11_spmd.sunk | while | flops 136315008 | bytes 9766151 | solution.py:122
  210.5 4.9 %bitcast_select_fusion.3 = f32[4,128,2048]{1,2,0:T(8,128)} fusion(f32[4,128,2048]{1,2,0:T(8,128)} %get-tuple-element.531, bf16[128,4,64]{0,2,1:T(8,128)(2,1)S(1)} %get-tuple-element.544, pred[128]{0:T(512)(128)(4,1)S(1)} %broadcast_compare_fusion.4, bf16[2048,128]{0,1:T(8,128)(2,1)S(1)} %dynamic-slice_bitcast_fusion.12), kind=kOutput, calls=%fused_computation.4.clone.1 | convolution fusion | flops 136314880 | bytes 8716800 | tf_op jit(solution)/shard_map/while/body/eval_jaxpr/while/body/rhd,md->hrm/dot_general | solution.py:115
  215.4 5.4 %copy.49 = f32[4,128,2048]{2,1,0:T(8,128)} copy(f32[4,128,2048]{1,2,0:T(8,128)} %get-tuple-element.503) | data formatting | bytes 8388608 | tf_op jit(solution)/shard_map/while/body/eval_jaxpr/while | solution.py:122
  228.2 8.6 %while.40 = (s32[]{:T(128)}, f32[128,4,64]{0,2,1:T(8,128)S(1)}, s32[]{:T(128)}, bf16[5,2048,128]{1,2,0:T(8,128)(2,1)}, s32[128]{0:T(128)S(1)}, /*index=5*/bf16[4...) while((s32[]{:T(128)}, f32[128,4,64]{0,2,1:T(8,128)S(1)}, s32[]{:T(128)}, ...), condition=%wide.region_16.16_spmd, body=%wide.region_15.15_spmd.sunk | while | flops 135299200 | bytes 3671303 | solution.py:165
  241.2 12.1 %while.39 = (s32[]{:T(128)}, f32[4,128,2048]{1,2,0:T(8,128)}, s32[]{:T(128)}, s32[128]{0:T(128)S(1)}, bf16[5,2048,128]{1,2,0:T(8,128)(2,1)}, /*index=5*/bf16[128...) while((s32[]{:T(128)}, f32[4,128,2048]{1,2,0:T(8,128)}, s32[]{:T(128)}, s32[128]{0:T(128)S(1)}, ...), condition=%wide.region_12.12_spmd, body=%wide.region_11.11_spmd.sunk | while | flops 136315008 | bytes 9766151 | solution.py:122
  242.3 4.9 %bitcast_select_fusion.3 = f32[4,128,2048]{1,2,0:T(8,128)} fusion(f32[4,128,2048]{1,2,0:T(8,128)} %get-tuple-element.531, bf16[128,4,64]{0,2,1:T(8,128)(2,1)S(1)} %get-tuple-element.544, pred[128]{0:T(512)(128)(4,1)S(1)} %broadcast_compare_fusion.4, bf16[2048,128]{0,1:T(8,128)(2,1)S(1)} %dynamic-slice_bitcast_fusion.12), kind=kOutput, calls=%fused_computation.4.clone.1 | convolution fusion | flops 136314880 | bytes 8716800 | tf_op jit(solution)/shard_map/while/body/eval_jaxpr/while/body/rhd,md->hrm/dot_general | solution.py:115
  248.3 4.9 %bitcast_select_fusion.3 = f32[4,128,2048]{1,2,0:T(8,128)} fusion(f32[4,128,2048]{1,2,0:T(8,128)} %get-tuple-element.531, bf16[128,4,64]{0,2,1:T(8,128)(2,1)S(1)} %get-tuple-element.544, pred[128]{0:T(512)(128)(4,1)S(1)} %broadcast_compare_fusion.4, bf16[2048,128]{0,1:T(8,128)(2,1)S(1)} %dynamic-slice_bitcast_fusion.12), kind=kOutput, calls=%fused_computation.4.clone.1 | convolution fusion | flops 136314880 | bytes 8716800 | tf_op jit(solution)/shard_map/while/body/eval_jaxpr/while/body/rhd,md->hrm/dot_general | solution.py:115
  253.3 5.4 %copy.49 = f32[4,128,2048]{2,1,0:T(8,128)} copy(f32[4,128,2048]{1,2,0:T(8,128)} %get-tuple-element.503) | data formatting | bytes 8388608 | tf_op jit(solution)/shard_map/while/body/eval_jaxpr/while | solution.py:122
  266.0 16.5 %while.40 = (s32[]{:T(128)}, f32[128,4,64]{0,2,1:T(8,128)S(1)}, s32[]{:T(128)}, bf16[5,2048,128]{1,2,0:T(8,128)(2,1)}, s32[128]{0:T(128)S(1)}, /*index=5*/bf16[4...) while((s32[]{:T(128)}, f32[128,4,64]{0,2,1:T(8,128)S(1)}, s32[]{:T(128)}, ...), condition=%wide.region_16.16_spmd, body=%wide.region_15.15_spmd.sunk | while | flops 135299200 | bytes 3671303 | solution.py:165
  287.0 6.0 %while.39 = (s32[]{:T(128)}, f32[4,128,2048]{1,2,0:T(8,128)}, s32[]{:T(128)}, s32[128]{0:T(128)S(1)}, bf16[5,2048,128]{1,2,0:T(8,128)(2,1)}, /*index=5*/bf16[128...) while((s32[]{:T(128)}, f32[4,128,2048]{1,2,0:T(8,128)}, s32[]{:T(128)}, s32[128]{0:T(128)S(1)}, ...), condition=%wide.region_12.12_spmd, body=%wide.region_11.11_spmd.sunk | while | flops 136315008 | bytes 9766151 | solution.py:122
  288.1 4.9 %bitcast_select_fusion.3 = f32[4,128,2048]{1,2,0:T(8,128)} fusion(f32[4,128,2048]{1,2,0:T(8,128)} %get-tuple-element.531, bf16[128,4,64]{0,2,1:T(8,128)(2,1)S(1)} %get-tuple-element.544, pred[128]{0:T(512)(128)(4,1)S(1)} %broadcast_compare_fusion.4, bf16[2048,128]{0,1:T(8,128)(2,1)S(1)} %dynamic-slice_bitcast_fusion.12), kind=kOutput, calls=%fused_computation.4.clone.1 | convolution fusion | flops 136314880 | bytes 8716800 | tf_op jit(solution)/shard_map/while/body/eval_jaxpr/while/body/rhd,md->hrm/dot_general | solution.py:115
  293.0 5.4 %copy.49 = f32[4,128,2048]{2,1,0:T(8,128)} copy(f32[4,128,2048]{1,2,0:T(8,128)} %get-tuple-element.503) | data formatting | bytes 8388608 | tf_op jit(solution)/shard_map/while/body/eval_jaxpr/while | solution.py:122
  305.8 8.6 %while.40 = (s32[]{:T(128)}, f32[128,4,64]{0,2,1:T(8,128)S(1)}, s32[]{:T(128)}, bf16[5,2048,128]{1,2,0:T(8,128)(2,1)}, s32[128]{0:T(128)S(1)}, /*index=5*/bf16[4...) while((s32[]{:T(128)}, f32[128,4,64]{0,2,1:T(8,128)S(1)}, s32[]{:T(128)}, ...), condition=%wide.region_16.16_spmd, body=%wide.region_15.15_spmd.sunk | while | flops 135299200 | bytes 3671303 | solution.py:165
  318.8 6.0 %while.39 = (s32[]{:T(128)}, f32[4,128,2048]{1,2,0:T(8,128)}, s32[]{:T(128)}, s32[128]{0:T(128)S(1)}, bf16[5,2048,128]{1,2,0:T(8,128)(2,1)}, /*index=5*/bf16[128...) while((s32[]{:T(128)}, f32[4,128,2048]{1,2,0:T(8,128)}, s32[]{:T(128)}, s32[128]{0:T(128)S(1)}, ...), condition=%wide.region_12.12_spmd, body=%wide.region_11.11_spmd.sunk | while | flops 136315008 | bytes 9766151 | solution.py:122
  319.9 4.9 %bitcast_select_fusion.3 = f32[4,128,2048]{1,2,0:T(8,128)} fusion(f32[4,128,2048]{1,2,0:T(8,128)} %get-tuple-element.531, bf16[128,4,64]{0,2,1:T(8,128)(2,1)S(1)} %get-tuple-element.544, pred[128]{0:T(512)(128)(4,1)S(1)} %broadcast_compare_fusion.4, bf16[2048,128]{0,1:T(8,128)(2,1)S(1)} %dynamic-slice_bitcast_fusion.12), kind=kOutput, calls=%fused_computation.4.clone.1 | convolution fusion | flops 136314880 | bytes 8716800 | tf_op jit(solution)/shard_map/while/body/eval_jaxpr/while/body/rhd,md->hrm/dot_general | solution.py:115
  324.9 5.4 %copy.49 = f32[4,128,2048]{2,1,0:T(8,128)} copy(f32[4,128,2048]{1,2,0:T(8,128)} %get-tuple-element.503) | data formatting | bytes 8388608 | tf_op jit(solution)/shard_map/while/body/eval_jaxpr/while | solution.py:122
  337.6 8.6 %while.40 = (s32[]{:T(128)}, f32[128,4,64]{0,2,1:T(8,128)S(1)}, s32[]{:T(128)}, bf16[5,2048,128]{1,2,0:T(8,128)(2,1)}, s32[128]{0:T(128)S(1)}, /*index=5*/bf16[4...) while((s32[]{:T(128)}, f32[128,4,64]{0,2,1:T(8,128)S(1)}, s32[]{:T(128)}, ...), condition=%wide.region_16.16_spmd, body=%wide.region_15.15_spmd.sunk | while | flops 135299200 | bytes 3671303 | solution.py:165
  351.3 42.0 %reduce-scatter.2.cloned.1.call-done = f32[768,256]{1,0:T(8,128)} async-done(((f32[768,2048]{1,0:T(8,128)}), f32[768,256]{1,0:T(8,128)}) %reduce-scatter.2.cloned.1.call-update) | async-done | bytes 786448 | tf_op jit(solution)/shard_map/reduce_scatter | solution.py:184
  (215 shorter events, 147.5 us)
Async XLA Ops:
  6.5 16.9 %copy-start = (bf16[2048,4,128]{2,1,0:T(4,128)(2,1)S(1)}, bf16[2048,4,128]{2,1,0:T(4,128)(2,1)}, u32[]{:S(2)}) copy-start(bf16[2048,4,128]{2,1,0:T(4,128)(2,1)} %param.18) | copy-start | bytes 6291460
  6.5 8.7 %copy-start.6 = (s32[80]{0:T(128)S(1)}, s32[80]{0:T(128)}, u32[]{:S(2)}) copy-start(s32[80]{0:T(128)} %param.23) | copy-start | bytes 964
  6.5 9.1 %copy-start.4 = (s32[80]{0:T(128)S(1)}, s32[80]{0:T(128)}, u32[]{:S(2)}) copy-start(s32[80]{0:T(128)} %param.22) | copy-start | bytes 964
  6.5 82.5 %all-gather.3.cloned.1.call-start = ((), (), s32[]{:S(2)}) async-start(), calls=%async_computation.2 | async-start | bytes 8912896 | tf_op jit(solution)/shard_map/all_gather | solution.py:94
  12.1 7.4 %copy-start.5 = (f32[2048]{0:T(1024)S(1)}, f32[2048]{0:T(1024)}, u32[]{:S(2)}) copy-start(f32[2048]{0:T(1024)} %param.16) | copy-start | bytes 24580
  15.2 378.2 %reduce-scatter.2.cloned.1.call-start = ((), (), s32[]{:S(2)}) async-start(), calls=%async_computation.1 | async-start | bytes 7077888 | tf_op jit(solution)/shard_map/reduce_scatter | solution.py:184
  15.9 3.5 copy-start.2
  95.0 4.5 %copy-start.3 = (bf16[6,128,256]{2,1,0:T(8,128)(2,1)S(1)}, bf16[6,128,256]{2,1,0:T(8,128)(2,1)}, u32[]{:S(2)}) copy-start(bf16[6,128,256]{2,1,0:T(8,128)(2,1)} %custom-call.4) | copy-start | bytes 1179652
  121.7 3.6 copy-start.1
  173.5 3.6 copy-start.1
  221.2 3.6 copy-start.1
  259.1 3.6 copy-start.1
  298.8 3.6 copy-start.1
  330.6 3.6 copy-start.1
Sparse Core Ops, SparseCore 0:
  15.3 73.6 all-gather.2
  351.4 41.8 reduce-scatter.1
where the time goes:
time: 405 us; the launch traced here: 402 us
  waiting for transfers between devices  103 us (25%)
  matrix products  90.3 us (22%)
  local copies, waits for them, and re-layouts  88.1 us (22%)
  other arithmetic  56.7 us (14%)
  loops' own time  50.1 us (12%)
  between operations  13.6 us (3%)
    all_gather x1, waiting for transfers between devices, body(): gathered = lax.all_gather(outgoing, 'seq', axis=0, tiled=True)  61.2 us
    dot_general x10, matrix products, add_scores(): jnp.einsum('rhd,md->hrm', block_query, keys_here, preferred_element_type=...  49.3 us
    reduce_scatter x1, waiting for transfers between devices, body(): lax.psum_scatter(partial_terms, 'tensor', scatter_dimension=1, tiled=True)  42 us
    another operation x6, loops' own time, one_block(): lax.fori_loop(first_request, last_request + 1, add_values, weighted)  41.6 us
    while x6, local copies, waits for them, and re-layouts, one_block(): lax.fori_loop(first_request, last_request + 1, add_scores, jnp.zeros((res...  32.3 us
    dot_general x10, matrix products, add_values(): jnp.einsum('hrm,md->rhd', chosen, values_here, preferred_element_type=jnp...  24.2 us
    reduce_max x6, other arithmetic, one_block(): jnp.max(jnp.where(prefix_mask[None], prefix_scores, MASKED_SCORE), axis=2)  17.2 us
    reduce_sum x12, other arithmetic, one_block(): row_total = jnp.sum(prefix_raw, axis=2) + jnp.sum(suffix_raw, axis=2)  16.5 us
  transfers between devices with their start and end apart: 2, of which 2 were waited for; matrix products, arithmetic and copies ran while one was open for 3% of the time, Pallas kernels for 0%

commit v1 on v0

v1 whole, which is shorter than its diff:
```python
import math

import jax
import jax.numpy as jnp
from jax import lax
from jax.sharding import PartitionSpec as P
from jax.experimental import pallas as pl
from jax.experimental.pallas import tpu as pltpu

QUERY_HEADS = 32
KEY_VALUE_HEADS = 4
HEAD_SIZE = 64
WINDOW_LENGTH = 2048
DEVICE_REQUESTS = 5
PPG = 64
WP = 16


MASKED_SCORE = -1e30


def normalize(tokens, norm_gain):
    widened = tokens.astype(jnp.float32)
    factor = lax.rsqrt(jnp.mean(widened * widened, axis=-1, keepdims=True) + 1e-05)
    return (widened * factor * norm_gain).astype(jnp.bfloat16)


def row_layout(lengths, row_total_count):
    request_ends = jnp.cumsum(lengths)
    starts = request_ends - lengths
    slot_ids = lax.iota(jnp.int32, row_total_count)
    row_request = jnp.sum((slot_ids[:, None] >= request_ends[None, :]).astype(jnp.int32), axis=1)
    row_live = slot_ids < request_ends[-1]
    choose = row_request[:, None] == lax.iota(jnp.int32, lengths.shape[0])[None, :]
    begins = jnp.sum(jnp.where(choose, starts[None, :], 0), axis=1)
    return (row_request, row_live, slot_ids - begins)


def lookup_rows(table, wanted):
    table_rows = table.shape[0]
    matches = wanted[:, None] == lax.iota(jnp.int32, table_rows)[None, :]
    return jnp.sum(jnp.where(matches[:, :, None], table[None, :, :], 0), axis=1)


def body(
    tokens,
    norm_gain,
    query_weight,
    key_value_matrix,
    out_weight,
    cache_pages,
    page_table,
    request_lengths,
    request_groups,
):
    seq_count = lax.axis_size("seq")
    seq_index = lax.axis_index("seq")
    tensor_rank_index = lax.axis_index("tensor")
    row_count = tokens.shape[0]
    resident_heads = query_weight.shape[1] // HEAD_SIZE
    key_value_head = tensor_rank_index * resident_heads // (QUERY_HEADS // KEY_VALUE_HEADS)
    group_count = page_table.shape[0]
    per_owner = WP // seq_count
    pages_here = cache_pages.shape[0]
    score_scale = HEAD_SIZE ** (-0.5)
    normed = normalize(tokens, norm_gain)
    query_rows = jnp.dot(normed, query_weight, preferred_element_type=jnp.float32).astype(
        jnp.bfloat16
    )
    query_rows = query_rows.reshape(row_count, resident_heads, HEAD_SIZE)
    head_weight = lax.dynamic_index_in_dim(key_value_matrix, key_value_head, 1, keepdims=False)
    new_token_rows = jnp.dot(normed, head_weight, preferred_element_type=jnp.float32).astype(
        jnp.bfloat16
    )
    lengths = lax.dynamic_slice_in_dim(
        request_lengths, seq_index * DEVICE_REQUESTS, DEVICE_REQUESTS
    )
    my_groups = lax.dynamic_slice_in_dim(
        request_groups, seq_index * DEVICE_REQUESTS, DEVICE_REQUESTS
    )
    tail_ids = page_table[:, PPG - WP :]
    holder = tail_ids // pages_here
    local_slot = tail_ids % pages_here
    earlier = lax.iota(jnp.int32, WP)[:, None] > lax.iota(jnp.int32, WP)[None, :]
    same_owner = holder[:, :, None] == holder[:, None, :]
    tail_rank = jnp.sum((same_owner & earlier[None, :, :]).astype(jnp.int32), axis=2)
    tail_hit = (holder == seq_index)[:, :, None] & (
        tail_rank[:, :, None] == lax.iota(jnp.int32, per_owner)[None, None, :]
    )
    tail_pick = jnp.sum(jnp.where(tail_hit, local_slot[:, :, None], 0), axis=1)
    head_pages = lax.dynamic_index_in_dim(cache_pages, key_value_head, 1, keepdims=False)
    my_holder = lookup_rows(holder, my_groups)
    my_rank = lookup_rows(tail_rank, my_groups)
    outgoing = head_pages[tail_pick.reshape(-1)]
    gathered = lax.all_gather(outgoing, "seq", axis=0, tiled=True)
    where_from = my_holder * (group_count * per_owner) + my_groups[:, None] * per_owner + my_rank
    window_rows = gathered[where_from.reshape(-1)]
    window_rows = window_rows.reshape(DEVICE_REQUESTS, WINDOW_LENGTH, 2 * HEAD_SIZE)
    starts = jnp.cumsum(lengths) - lengths
    bounds = jnp.concatenate([starts, starts + lengths]).astype(jnp.int32)
    fresh_pad = new_token_rows
    query_pad = jnp.concatenate(
        [query_rows, jnp.zeros_like(query_rows)], axis=-1
    ).transpose(1, 0, 2)
    attended = attend(bounds, query_pad, window_rows, fresh_pad)
    gathered_heads = lax.all_gather(attended, "tensor", axis=0, tiled=True)
    columns = out_weight.shape[1] // lax.axis_size("tensor")
    my_columns = lax.dynamic_slice_in_dim(out_weight, tensor_rank_index * columns, columns, 1)
    my_columns = my_columns.reshape(gathered_heads.shape[0], HEAD_SIZE, columns)
    projected = jnp.einsum(
        "hrd,hdc->rc", gathered_heads, my_columns, preferred_element_type=jnp.float32
    )
    return projected.astype(jnp.bfloat16)


BLOCK_ROWS = 64


def attend_kernel(bounds_ref, q_ref, win_ref, fresh_ref, o_ref):
    heads, block_rows, _ = q_ref.shape
    stacked = heads * block_rows
    request_count = win_ref.shape[0]
    window = win_ref.shape[1]
    row_count = fresh_ref.shape[0]
    first_row = pl.program_id(0) * block_rows
    score_scale = HEAD_SIZE ** (-0.5)
    q = q_ref[...].reshape(stacked, 2 * HEAD_SIZE)
    rows = first_row + lax.broadcasted_iota(jnp.int32, (heads, block_rows, 1), 1).reshape(stacked, 1)
    r_first = jnp.int32(0)
    r_last = jnp.int32(-1)
    for k in range(request_count):
        r_first = r_first + (bounds_ref[request_count + k] <= first_row).astype(jnp.int32)
        r_last = r_last + (bounds_ref[k] < first_row + block_rows).astype(jnp.int32)
    r_last = jnp.minimum(r_last, request_count - 1)
    offsets = lax.broadcasted_iota(jnp.int32, (stacked, window), 1)
    column = lax.broadcasted_iota(jnp.int32, (stacked, row_count), 1)
    fresh = fresh_ref[...]

    def one_request(r, out_acc):
        begin = bounds_ref[r]
        finish = bounds_ref[request_count + r]
        in_request = (rows >= begin) & (rows < finish)
        threshold = jnp.where(in_request, rows - begin + 1, window)
        newest = jnp.where(in_request, rows, -1)
        keys = win_ref[r]
        prefix_scores = lax.dot_general(
            q, keys, (((1,), (1,)), ((), ())), preferred_element_type=jnp.float32
        ) * score_scale
        suffix_scores = lax.dot_general(
            q, fresh, (((1,), (1,)), ((), ())), preferred_element_type=jnp.float32
        ) * score_scale
        prefix_mask = offsets >= threshold
        suffix_mask = (
            (column >= begin) & (column <= newest) & (rows - column < WINDOW_LENGTH)
        )
        top = jnp.maximum(
            jnp.max(jnp.where(prefix_mask, prefix_scores, MASKED_SCORE), axis=1, keepdims=True),
            jnp.max(jnp.where(suffix_mask, suffix_scores, MASKED_SCORE), axis=1, keepdims=True),
        )
        prefix_raw = jnp.where(prefix_mask, jnp.exp(prefix_scores - top), 0.0)
        suffix_raw = jnp.where(suffix_mask, jnp.exp(suffix_scores - top), 0.0)
        total = jnp.sum(prefix_raw, axis=1, keepdims=True) + jnp.sum(
            suffix_raw, axis=1, keepdims=True
        )
        weighted = jnp.dot(
            prefix_raw.astype(jnp.bfloat16), keys, preferred_element_type=jnp.float32
        ) + jnp.dot(suffix_raw.astype(jnp.bfloat16), fresh, preferred_element_type=jnp.float32)
        safe_total = jnp.where(in_request, total, 1.0)
        return jnp.where(in_request, weighted / safe_total, out_acc)

    out_acc = lax.fori_loop(
        r_first, r_last + 1, one_request, jnp.zeros((stacked, 2 * HEAD_SIZE), jnp.float32)
    )
    o_ref[...] = out_acc[:, HEAD_SIZE:].astype(o_ref.dtype).reshape(heads, block_rows, HEAD_SIZE)


def attend(bounds, query_pad, window_rows, fresh_rows):
    heads, row_count, width = query_pad.shape
    block_rows = math.gcd(row_count, BLOCK_ROWS)
    requests, window, _ = window_rows.shape
    return pl.pallas_call(
        attend_kernel,
        out_shape=jax.ShapeDtypeStruct((heads, row_count, HEAD_SIZE), jnp.bfloat16),
        grid_spec=pltpu.PrefetchScalarGridSpec(
            num_scalar_prefetch=1,
            grid=(row_count // block_rows,),
            in_specs=[
                pl.BlockSpec((heads, block_rows, width), lambda i, b: (0, i, 0)),
                pl.BlockSpec((requests, window, width), lambda i, b: (0, 0, 0)),
                pl.BlockSpec((row_count, width), lambda i, b: (0, 0)),
            ],
            out_specs=pl.BlockSpec((heads, block_rows, HEAD_SIZE), lambda i, b: (0, i, 0)),
        ),
        compiler_params=pltpu.CompilerParams(
            dimension_semantics=("arbitrary",), vmem_limit_bytes=48 * 1024 * 1024
        ),
    )(bounds, query_pad, window_rows, fresh_rows)


def solution(mesh):
    return jax.shard_map(
        body,
        mesh=mesh,
        in_specs=(
            P("seq", None),
            P(),
            P(None, "tensor"),
            P(),
            P(),
            P("seq", None, None, None),
            P(),
            P(),
            P(),
        ),
        out_specs=P("seq", "tensor"),
        check_vma=False,
    )
```

time: 405 us -> 172 us (0.42)
  matrix products: 90.3 us -> 7.27 us
  local copies, waits for them, and re-layouts: 88.1 us -> 22.4 us
  other arithmetic: 56.7 us -> 5.57 us
  loops' own time: 50.1 us -> 0 us
  Pallas kernels: 0 us -> 31.5 us
  waiting for transfers between devices: 103 us -> 90.8 us
    dot_general x33 -> x1, matrix products: 84.8 us -> 3.66 us  [body(): jnp.einsum('hrd,hdc->rc', gathered_heads, my_columns, preferred_element_t...]
    another operation x13 -> x0, loops' own time: 50.1 us -> none  [the longest x6 41.6 us: one_block(): lax.fori_loop(first_request, last_request + 1, add_values, weighted)]
    reduce_scatter x1 -> x0, waiting for transfers between devices: 42 us -> none  [body(): lax.psum_scatter(partial_terms, 'tensor', scatter_dimension=1, tiled=True)]
    while x18 -> x0, local copies, waits for them, and re-layouts: 32.4 us -> none  [the longest x6 32.3 us: one_block(): lax.fori_loop(first_request, last_request + 1, add_scores, jnp.zeros((res...]
    pallas_call x0 -> x1, Pallas kernels: none -> 31.5 us  [attend(): pl.pallas_call(attend_kernel, out_shape=jax.ShapeDtypeStruct((heads, row_...]
    all_gather x0 -> x1, waiting for transfers between devices: none -> 28.1 us  [body(): gathered_heads = lax.all_gather(attended, 'tensor', axis=0, tiled=True)]
    squeeze x26 -> x0, local copies, waits for them, and re-layouts: 21.7 us -> none  [the longest x10 10.9 us: add_values(): lax.dynamic_index_in_dim(window_rows, request_slot, 0, keepdims=False)]
    reduce_max x12 -> x0, other arithmetic: 21.4 us -> none  [the longest x6 17.2 us: one_block(): jnp.max(jnp.where(prefix_mask[None], prefix_scores, MASKED_SCORE), axis=2)]
  transfers between devices with their start and end apart: 2 -> 2, of which waited for: 2 -> 2; matrix products, arithmetic and copies ran while one was open for 3% -> 7% of each run, Pallas kernels for 0% -> 0%
where the time goes in v1:
time: 172 us; the launch traced here: 171 us
  waiting for transfers between devices  90.8 us (53%)
  Pallas kernels  31.5 us (18%)
  local copies, waits for them, and re-layouts  22.4 us (13%)
  between operations  13.6 us (8%)
  matrix products  7.27 us (4%)
  other arithmetic  5.57 us (3%)
    all_gather x1, waiting for transfers between devices, body(): gathered = lax.all_gather(outgoing, 'seq', axis=0, tiled=True)  62.7 us
    pallas_call x1, Pallas kernels, attend(): pl.pallas_call(attend_kernel, out_shape=jax.ShapeDtypeStruct((heads, row_...  31.5 us
    all_gather x1, waiting for transfers between devices, body(): gathered_heads = lax.all_gather(attended, 'tensor', axis=0, tiled=True)  28.1 us
    gather x1, local copies, waits for them, and re-layouts, body(): window_rows = gathered[where_from.reshape(-1)]  5.99 us
    dot_general x1, matrix products, body(): jnp.einsum('hrd,hdc->rc', gathered_heads, my_columns, preferred_element_t...  3.66 us
  transfers between devices with their start and end apart: 2, of which 2 were waited for; matrix products, arithmetic and copies ran while one was open for 7% of the time, Pallas kernels for 0%

profile of v1, /device:TPU:1, one launch (start us, length us, event | category | flops | bytes accessed | tf_op | source)
XLA Modules:
  0.0 171.1 jit_solution(9068111090463244274)
XLA Ops:
  6.6 0.9 add_select_fusion.1
  7.5 0.4 convert_reduce_fusion
  7.9 0.9 fusion.7
  8.9 3.2 %dynamic-slice_bitcast_fusion = bf16[64,128,128]{2,1,0:T(8,128)(2,1)} fusion(bf16[64,4,128,128]{3,2,1,0:T(8,128)(2,1)} %param.14, s32[]{:T(128)S(6)} %select_n.63), kind=kLoop, calls=%fused_computation.7 | loop fusion | bytes 4194308 | tf_op jit(solution)/shard_map/jit(dynamic_index_in_dim)/squeeze | solution.py:91
  12.1 3.0 %gather_fusion = bf16[16,128,128]{2,1,0:T(8,128)(2,1)} fusion(bf16[64,128,128]{2,1,0:T(8,128)(2,1)} %dynamic-slice_bitcast_fusion, s32[1024]{0:T(1024)S(1)} %pad_clamp_fusion.1), kind=kCustom, calls=%fused_computation | custom fusion | bytes 1048640 | tf_op jit(solution)/shard_map/gather | solution.py:94
  15.1 0.0 all-gather.4.cloned.1.call-start
  15.2 0.1 dynamic_slice.19
  15.3 0.1 iota_compare_fusion.1
  15.3 0.1 select_reduce_fusion.1
  15.4 0.1 add_add_fusion
  15.5 0.1 add.95
  15.6 0.1 dynamic-slice_bitcast_fusion.1
  15.7 0.2 reduce-window.9
  15.9 2.7 %fusion = f32[768]{0:T(1024)S(1)} fusion(bf16[768,2048]{1,0:T(8,128)(2,1)} %param.9), kind=kLoop, calls=%fused_computation.4 | loop fusion | flops 4717824 | bytes 3148800 | tf_op jit(solution)/shard_map/reduce_sum | solution.py:24
  18.6 0.1 copy-done.3
  18.7 2.6 %convolution_convert_fusion = bf16[768,256]{0,1:T(8,128)(2,1)S(1)} fusion(bf16[2048,256]{1,0:T(8,128)(2,1)} %param.11, bf16[768,2048]{1,0:T(8,128)(2,1)S(1)} %copy-done.3, f32[2048]{0:T(1024)S(1)} %copy-done.6, f32[768]{0:T(1024)S(1)} %add_rsqrt_fusion), kind=kOutput, calls=%fused_computation.10 | convolution fusion | flops 811794432 | bytes 4598784 | tf_op jit(solution)/shard_map/dot_general | solution.py:67
  21.3 1.2 copy.17
  22.5 0.1 dynamic-slice_subtract_fusion
  22.6 0.1 pad_add_fusion.bounds_ref
  22.7 1.4 pad_bitcast_fusion.q_ref
  24.1 1.1 constant_dynamic-slice_fusion.1
  25.3 1.0 convolution_convert_fusion.1.fresh_ref
  26.3 62.7 %all-gather.6.cloned.1.call-done = bf16[256,128,128]{2,1,0:T(8,128)(2,1)} async-done(((bf16[16,128,128]{2,1,0:T(8,128)(2,1)}), bf16[256,128,128]{2,1,0:T(8,128)(2,1)}) %all-gather.6.cloned.1.call-update) | async-done | bytes 8388624 | tf_op jit(solution)/shard_map/all_gather | solution.py:95
  89.0 6.0 %gather_fusion.1 = bf16[80,128,128]{2,1,0:T(8,128)(2,1)} fusion(bf16[256,128,128]{2,1,0:T(8,128)(2,1)} %all-gather.6.cloned.1.call-done, s32[1024]{0:T(1024)S(1)} %pad_clamp_fusion), kind=kCustom, calls=%fused_computation.1 | custom fusion | bytes 5243200 | tf_op jit(solution)/shard_map/gather | solution.py:97
  95.0 1.7 %copy-done.1 = bf16[80,128,128]{2,1,0:T(8,128)(2,1)S(1)} copy-done((bf16[80,128,128]{2,1,0:T(8,128)(2,1)S(1)}, bf16[80,128,128]{2,1,0:T(8,128)(2,1)}, u32[]{:S(2)}) %copy-start.1) | copy-done | bytes 2621464
  96.7 31.5 %shard_map.91 = bf16[4,768,64]{2,1,0:T(8,128)(2,1)S(1)} custom-call(s32[10]{0:T(128)S(1)} %pad_add_fusion.bounds_ref, bf16[4,768,128]{2,1,0:T(8,128)(2,1)S(1)} %pad_bitcast_fusion.q_ref, bf16[5,2048,128]{2,1,0:T(8,128)(2,1)S(1)} %bitcast.27, bf16[768,128]{1,0:T(8,128)(2,1)S(1)} %convolution_convert_fusion.1.fresh_ref), custom_call_target="tpu_custom_call" | custom-call | tf_op jit(solution)/shard_map/pallas_call | solution.py:181
  128.2 0.9 copy-done.2
  129.1 2.1 %copy.19 = bf16[4,768,64]{1,2,0:T(8,128)(2,1)} copy(bf16[4,768,64]{2,1,0:T(8,128)(2,1)} %copy-done.2) | data formatting | bytes 786432 | tf_op jit(solution)/shard_map/pallas_call | solution.py:181
  131.3 0.0 all-gather.4.cloned.1.call-update
  131.3 1.3 constant_dynamic-slice_fusion
  132.6 28.1 %all-gather.4.cloned.1.call-done = bf16[32,768,64]{1,2,0:T(8,128)(2,1)} async-done(((bf16[4,768,64]{1,2,0:T(8,128)(2,1)}), bf16[32,768,64]{1,2,0:T(8,128)(2,1)}) %all-gather.4.cloned.1.call-update) | async-done | bytes 3145744 | tf_op jit(solution)/shard_map/all_gather | solution.py:106
  160.6 3.7 %fusion.3 = bf16[768,256]{1,0:T(8,128)(2,1)} fusion(bf16[32,768,64]{1,2,0:T(8,128)(2,1)} %all-gather.4.cloned.1.call-done, bf16[32,64,256]{2,1,0:T(8,128)(2,1)S(1)} %bitcast.28), kind=kOutput, calls=%fused_computation.9 | convolution fusion | flops 805502976 | bytes 4587520 | tf_op jit(solution)/shard_map/hrd,hdc->rc/dot_general | solution.py:110
  (21 shorter events, 0.1 us)
Async XLA Ops:
  6.5 17.6 %copy-start = (bf16[2048,4,128]{2,1,0:T(4,128)(2,1)S(1)}, bf16[2048,4,128]{2,1,0:T(4,128)(2,1)}, u32[]{:S(2)}) copy-start(bf16[2048,4,128]{2,1,0:T(4,128)(2,1)} %param.12) | copy-start | bytes 6291460
  6.5 8.6 %copy-start.7 = (s32[80]{0:T(128)S(1)}, s32[80]{0:T(128)}, u32[]{:S(2)}) copy-start(s32[80]{0:T(128)} %param.17) | copy-start | bytes 964
  6.5 9.1 %copy-start.5 = (s32[80]{0:T(128)S(1)}, s32[80]{0:T(128)}, u32[]{:S(2)}) copy-start(s32[80]{0:T(128)} %param.16) | copy-start | bytes 964
  6.5 82.4 %all-gather.6.cloned.1.call-start = ((), (), s32[]{:S(2)}) async-start(), calls=%async_computation.1 | async-start | bytes 8912896 | tf_op jit(solution)/shard_map/all_gather | solution.py:95
  12.1 6.5 %copy-start.6 = (f32[2048]{0:T(1024)S(1)}, f32[2048]{0:T(1024)}, u32[]{:S(2)}) copy-start(f32[2048]{0:T(1024)} %param.10) | copy-start | bytes 24580
  15.1 145.5 %all-gather.4.cloned.1.call-start = ((), (), s32[]{:S(2)}) async-start(), calls=%async_computation | async-start | bytes 3538944 | tf_op jit(solution)/shard_map/all_gather | solution.py:106
  15.9 2.8 %copy-start.3 = (bf16[768,2048]{1,0:T(8,128)(2,1)S(1)}, bf16[768,2048]{1,0:T(8,128)(2,1)}, u32[]{:S(2)}) copy-start(bf16[768,2048]{1,0:T(8,128)(2,1)} %param.9) | copy-start | bytes 9437188
  22.5 2.8 %copy-start.4 = (bf16[768,2048]{1,0:T(8,128)(2,1)S(1)}, bf16[768,2048]{1,0:T(8,128)(2,1)}, u32[]{:S(2)}) copy-start(bf16[768,2048]{1,0:T(8,128)(2,1)} %param.9) | copy-start | bytes 9437188
  95.0 1.7 %copy-start.1 = (bf16[80,128,128]{2,1,0:T(8,128)(2,1)S(1)}, bf16[80,128,128]{2,1,0:T(8,128)(2,1)}, u32[]{:S(2)}) copy-start(bf16[80,128,128]{2,1,0:T(8,128)(2,1)} %gather_fusion.1) | copy-start | bytes 7864324
  128.2 0.9 copy-start.2
Sparse Core Ops, SparseCore 0:
  15.2 73.6 all-gather.5
  131.4 29.2 all-gather.3

commit v2 on v1

--- a/solution.py
+++ b/solution.py
@@ -81,20 +81,13 @@
     tail_ids = page_table[:, PPG - WP :]
     holder = tail_ids // pages_here
     local_slot = tail_ids % pages_here
-    earlier = lax.iota(jnp.int32, WP)[:, None] > lax.iota(jnp.int32, WP)[None, :]
-    same_owner = holder[:, :, None] == holder[:, None, :]
-    tail_rank = jnp.sum((same_owner & earlier[None, :, :]).astype(jnp.int32), axis=2)
-    tail_hit = (holder == seq_index)[:, :, None] & (
-        tail_rank[:, :, None] == lax.iota(jnp.int32, per_owner)[None, None, :]
-    )
-    tail_pick = jnp.sum(jnp.where(tail_hit, local_slot[:, :, None], 0), axis=1)
+    held_slot = jnp.sum(jnp.where(holder == seq_index, local_slot, 0), axis=1)
+    all_groups = request_groups.reshape(seq_count, DEVICE_REQUESTS)
     head_pages = lax.dynamic_index_in_dim(cache_pages, key_value_head, 1, keepdims=False)
-    my_holder = lookup_rows(holder, my_groups)
-    my_rank = lookup_rows(tail_rank, my_groups)
-    outgoing = head_pages[tail_pick.reshape(-1)]
-    gathered = lax.all_gather(outgoing, "seq", axis=0, tiled=True)
-    where_from = my_holder * (group_count * per_owner) + my_groups[:, None] * per_owner + my_rank
-    window_rows = gathered[where_from.reshape(-1)]
+    outgoing = head_pages[held_slot[all_groups]]
+    incoming = lax.all_to_all(outgoing, "seq", 0, 0, tiled=True)
+    page_source = holder[my_groups]
+    window_rows = incoming[page_source, lax.iota(jnp.int32, DEVICE_REQUESTS)[:, None]]
     window_rows = window_rows.reshape(DEVICE_REQUESTS, WINDOW_LENGTH, 2 * HEAD_SIZE)
     starts = jnp.cumsum(lengths) - lengths
     bounds = jnp.concatenate([starts, starts + lengths]).astype(jnp.int32)

time: 172 us -> 144 us (0.84)
  waiting for transfers between devices: 90.8 us -> 54.5 us
  starting transfers between devices: 0.04 us -> 7.79 us
  local copies, waits for them, and re-layouts: 22.4 us -> 24.9 us
  Pallas kernels: 31.5 us -> 29.5 us
    all_gather x1 -> x0, waiting for transfers between devices: 62.7 us -> none  [body(): gathered = lax.all_gather(outgoing, 'seq', axis=0, tiled=True)]
    all_to_all x0 -> x1, waiting for transfers between devices: none -> 23.5 us  [body(): incoming = lax.all_to_all(outgoing, 'seq', 0, 0, tiled=True)]
    all_to_all x0 -> x1, starting transfers between devices: none -> 7.75 us  [body(): incoming = lax.all_to_all(outgoing, 'seq', 0, 0, tiled=True)]
    all_gather x1, waiting for transfers between devices: 28.1 us -> 31 us  [body(): gathered_heads = lax.all_gather(attended, 'tensor', axis=0, tiled=True)]
    pallas_call x1, Pallas kernels: 31.5 us -> 29.5 us  [attend(): pl.pallas_call(attend_kernel, out_shape=jax.ShapeDtypeStruct((heads, row_...]
    gather x2 -> x5, local copies, waits for them, and re-layouts: 9.02 us -> 10.6 us  [the longest x3 5.43 us: body(): outgoing = head_pages[held_slot[all_groups]]]
  transfers between devices with their start and end apart: 2 -> 2, of which waited for: 2 -> 2; matrix products, arithmetic and copies ran while one was open for 7% -> 9% of each run, Pallas kernels for 0% -> 0%
where the time goes in v2:
time: 144 us; the launch traced here: 142 us
  waiting for transfers between devices  54.5 us (38%)
  Pallas kernels  29.5 us (20%)
  local copies, waits for them, and re-layouts  24.9 us (17%)
  between operations  13.6 us (9%)
  starting transfers between devices  7.79 us (5%)
  matrix products  7.28 us (5%)
  other arithmetic  5 us (3%)
    all_gather x1, waiting for transfers between devices, body(): gathered_heads = lax.all_gather(attended, 'tensor', axis=0, tiled=True)  31 us
    pallas_call x1, Pallas kernels, attend(): pl.pallas_call(attend_kernel, out_shape=jax.ShapeDtypeStruct((heads, row_...  29.5 us
    all_to_all x1, waiting for transfers between devices, body(): incoming = lax.all_to_all(outgoing, 'seq', 0, 0, tiled=True)  23.5 us
    all_to_all x1, starting transfers between devices, body(): incoming = lax.all_to_all(outgoing, 'seq', 0, 0, tiled=True)  7.75 us
    gather x3, local copies, waits for them, and re-layouts, body(): outgoing = head_pages[held_slot[all_groups]]  5.43 us
    gather x1, local copies, waits for them, and re-layouts, body(): incoming[page_source, lax.iota(jnp.int32, DEVICE_REQUESTS)[:, None]]  4.64 us
    dot_general x1, matrix products, body(): jnp.einsum('hrd,hdc->rc', gathered_heads, my_columns, preferred_element_t...  3.66 us
    squeeze x1, local copies, waits for them, and re-layouts, body(): lax.dynamic_index_in_dim(cache_pages, key_value_head, 1, keepdims=False)  3.2 us
  transfers between devices with their start and end apart: 2, of which 2 were waited for; matrix products, arithmetic and copies ran while one was open for 9% of the time, Pallas kernels for 0%

profile of v2, /device:TPU:1, one launch (start us, length us, event | category | flops | bytes accessed | tf_op | source)
XLA Modules:
  0.0 142.4 jit_solution(4881843172450538901)
XLA Ops:
  6.5 0.9 add_select_fusion.1
  7.5 0.7 reshape.106
  8.2 0.1 reshape.111
  8.3 0.9 fusion.7
  9.2 1.2 gather_fusion
  10.5 0.1 gather.17
  10.5 0.1 reshape.119
  10.7 3.2 %dynamic-slice_bitcast_fusion = bf16[64,128,128]{2,1,0:T(8,128)(2,1)} fusion(bf16[64,4,128,128]{3,2,1,0:T(8,128)(2,1)} %param.14, s32[]{:T(128)S(6)} %select_n.69), kind=kLoop, calls=%fused_computation.9 | loop fusion | bytes 4194308 | tf_op jit(solution)/shard_map/jit(dynamic_index_in_dim)/squeeze | solution.py:86
  13.9 4.1 %gather_fusion.1 = bf16[80,128,128]{2,1,0:T(8,128)(2,1)} fusion(bf16[64,128,128]{2,1,0:T(8,128)(2,1)} %dynamic-slice_bitcast_fusion, s32[1024]{0:T(1024)S(1)} %pad_clamp_fusion.1), kind=kCustom, calls=%fused_computation.1 | custom fusion | bytes 5243200 | tf_op jit(solution)/shard_map/gather | solution.py:87
  18.0 7.7 %all-to-all-start = ((bf16[16,5,128,128]{3,2,1,0:T(8,128)(2,1)}), bf16[16,5,128,128]{3,2,1,0:T(8,128)(2,1)}, u32[]{:S(2)}, u32[]{:S(2)}) async-start(bf16[16,5,128,128]{3,2,1,0:T(8,128)(2,1)} %bitcast.31), calls=%async_computation | async-start | bytes 5242880 | tf_op jit(solution)/shard_map/all_to_all | solution.py:88
  25.8 0.1 compare_select_fusion.3
  25.9 0.6 gather_fusion.2
  26.5 0.1 reshape.133
  26.6 0.2 reduce-window.9
  26.8 2.7 %fusion = f32[768]{0:T(1024)S(1)} fusion(bf16[768,2048]{1,0:T(8,128)(2,1)} %param.9), kind=kLoop, calls=%fused_computation.6 | loop fusion | flops 4717824 | bytes 3148800 | tf_op jit(solution)/shard_map/reduce_sum | solution.py:24
  29.6 0.1 copy-done.3
  29.6 2.6 %convolution_convert_fusion = bf16[768,256]{0,1:T(8,128)(2,1)S(1)} fusion(bf16[2048,256]{1,0:T(8,128)(2,1)} %param.11, bf16[768,2048]{1,0:T(8,128)(2,1)S(1)} %copy-done.3, f32[2048]{0:T(1024)S(1)} %copy-done.7, f32[768]{0:T(1024)S(1)} %add_rsqrt_fusion), kind=kOutput, calls=%fused_computation.12 | convolution fusion | flops 811794432 | bytes 4598784 | tf_op jit(solution)/shard_map/dot_general | solution.py:67
  32.2 1.2 copy.14
  33.4 0.1 dynamic-slice_subtract_fusion
  33.5 0.1 pad_add_fusion.bounds_ref
  33.6 1.4 %pad_bitcast_fusion.q_ref = bf16[4,768,128]{2,1,0:T(8,128)(2,1)S(1)} fusion(bf16[768,4,64]{2,0,1:T(8,128)(2,1)} %copy.14), kind=kLoop, calls=%fused_computation.14 | loop fusion | bytes 1179648 | tf_op jit(solution)/shard_map/transpose | solution.py:97
  35.0 1.1 constant_dynamic-slice_fusion.1
  36.2 1.0 convolution_convert_fusion.1.fresh_ref
  37.2 23.5 %all-to-all-done = bf16[16,5,128,128]{3,2,1,0:T(8,128)(2,1)} async-done(((bf16[16,5,128,128]{3,2,1,0:T(8,128)(2,1)}), bf16[16,5,128,128]{3,2,1,0:T(8,128)(2,1)}, u32[]{:S(2)}, u32[]{:S(2)}) %all-to-all-start) | async-done | bytes 2621472 | tf_op jit(solution)/shard_map/all_to_all | solution.py:88
  60.7 4.6 %gather_fusion.3 = bf16[80,128,128]{2,1,0:T(8,128)(2,1)} fusion(bf16[16,5,128,128]{3,2,1,0:T(8,128)(2,1)} %all-to-all-done, s32[80]{0:T(128)S(1)} %reshape.133), kind=kCustom, calls=%fused_computation.3 | custom fusion | bytes 5243520 | tf_op jit(solution)/shard_map/gather | solution.py:90
  65.4 1.7 %copy-done.1 = bf16[80,128,128]{2,1,0:T(8,128)(2,1)S(1)} copy-done((bf16[80,128,128]{2,1,0:T(8,128)(2,1)S(1)}, bf16[80,128,128]{2,1,0:T(8,128)(2,1)}, u32[]{:S(2)}) %copy-start.1) | copy-done | bytes 2621464
  67.1 29.5 %shard_map.91 = bf16[4,768,64]{2,1,0:T(8,128)(2,1)S(1)} custom-call(s32[10]{0:T(128)S(1)} %pad_add_fusion.bounds_ref, bf16[4,768,128]{2,1,0:T(8,128)(2,1)S(1)} %pad_bitcast_fusion.q_ref, bf16[5,2048,128]{2,1,0:T(8,128)(2,1)S(1)} %bitcast.30, bf16[768,128]{1,0:T(8,128)(2,1)S(1)} %convolution_convert_fusion.1.fresh_ref), custom_call_target="tpu_custom_call" | custom-call | tf_op jit(solution)/shard_map/pallas_call | solution.py:174
  96.6 0.9 copy-done.2
  97.5 2.1 %copy.16 = bf16[4,768,64]{1,2,0:T(8,128)(2,1)} copy(bf16[4,768,64]{2,1,0:T(8,128)(2,1)} %copy-done.2) | data formatting | bytes 786432 | tf_op jit(solution)/shard_map/pallas_call | solution.py:174
  99.7 1.3 constant_dynamic-slice_fusion
  101.0 31.0 %all-gather.2.cloned.1.call-done = bf16[32,768,64]{1,2,0:T(8,128)(2,1)} async-done(((bf16[4,768,64]{1,2,0:T(8,128)(2,1)}), bf16[32,768,64]{1,2,0:T(8,128)(2,1)}) %all-gather.2.cloned.1.call-update) | async-done | bytes 3145744 | tf_op jit(solution)/shard_map/all_gather | solution.py:99
  131.9 3.7 %fusion.3 = bf16[768,256]{1,0:T(8,128)(2,1)} fusion(bf16[32,768,64]{1,2,0:T(8,128)(2,1)} %all-gather.2.cloned.1.call-done, bf16[32,64,256]{2,1,0:T(8,128)(2,1)S(1)} %bitcast.32), kind=kOutput, calls=%fused_computation.11 | convolution fusion | flops 805502976 | bytes 4587520 | tf_op jit(solution)/shard_map/hrd,hdc->rc/dot_general | solution.py:103
  (23 shorter events, 0.2 us)
Async XLA Ops:
  6.5 28.5 %copy-start = (bf16[2048,4,128]{2,1,0:T(4,128)(2,1)S(1)}, bf16[2048,4,128]{2,1,0:T(4,128)(2,1)}, u32[]{:S(2)}) copy-start(bf16[2048,4,128]{2,1,0:T(4,128)(2,1)} %param.12) | copy-start | bytes 6291460
  18.0 7.8 %copy-start.5 = (s32[80]{0:T(128)S(1)}, s32[80]{0:T(128)}, u32[]{:S(2)}) copy-start(s32[80]{0:T(128)} %param.17) | copy-start | bytes 964
  18.0 8.6 %copy-start.6 = (s32[80]{0:T(128)S(1)}, s32[80]{0:T(128)}, u32[]{:S(2)}) copy-start(s32[80]{0:T(128)} %param.16) | copy-start | bytes 964
  18.0 11.6 %copy-start.7 = (f32[2048]{0:T(1024)S(1)}, f32[2048]{0:T(1024)}, u32[]{:S(2)}) copy-start(f32[2048]{0:T(1024)} %param.10) | copy-start | bytes 24580
  18.0 42.8 %all-to-all-start = ((bf16[16,5,128,128]{3,2,1,0:T(8,128)(2,1)}), bf16[16,5,128,128]{3,2,1,0:T(8,128)(2,1)}, u32[]{:S(2)}, u32[]{:S(2)}) async-start(bf16[16,5,128,128]{3,2,1,0:T(8,128)(2,1)} %bitcast.31), calls=%async_computation | async-start | bytes 5242880 | tf_op jit(solution)/shard_map/all_to_all | solution.py:88
  25.7 106.2 %all-gather.2.cloned.1.call-start = ((), (), s32[]{:S(2)}) async-start(), calls=%async_computation.1 | async-start | bytes 3538944 | tf_op jit(solution)/shard_map/all_gather | solution.py:99
  26.8 2.8 %copy-start.3 = (bf16[768,2048]{1,0:T(8,128)(2,1)S(1)}, bf16[768,2048]{1,0:T(8,128)(2,1)}, u32[]{:S(2)}) copy-start(bf16[768,2048]{1,0:T(8,128)(2,1)} %param.9) | copy-start | bytes 9437188
  33.4 2.8 %copy-start.4 = (bf16[768,2048]{1,0:T(8,128)(2,1)S(1)}, bf16[768,2048]{1,0:T(8,128)(2,1)}, u32[]{:S(2)}) copy-start(bf16[768,2048]{1,0:T(8,128)(2,1)} %param.9) | copy-start | bytes 9437188
  65.4 1.7 %copy-start.1 = (bf16[80,128,128]{2,1,0:T(8,128)(2,1)S(1)}, bf16[80,128,128]{2,1,0:T(8,128)(2,1)}, u32[]{:S(2)}) copy-start(bf16[80,128,128]{2,1,0:T(8,128)(2,1)} %gather_fusion.3) | copy-start | bytes 7864324
  96.6 0.9 copy-start.2
Sparse Core Ops, SparseCore 0:
  99.8 32.1 all-gather.1

commit v3 on v2

--- a/solution.py
+++ b/solution.py
@@ -55,7 +55,8 @@
 ):
     seq_count = lax.axis_size("seq")
     seq_index = lax.axis_index("seq")
-    tensor_rank_index = lax.axis_index("tensor")
+    core_index = lax.axis_index("tc")
+    tensor_rank_index = lax.axis_index("tz") * lax.axis_size("tc") + core_index
     row_count = tokens.shape[0]
     resident_heads = query_weight.shape[1] // HEAD_SIZE
     key_value_head = tensor_rank_index * resident_heads // (QUERY_HEADS // KEY_VALUE_HEADS)
@@ -84,10 +85,17 @@
     held_slot = jnp.sum(jnp.where(holder == seq_index, local_slot, 0), axis=1)
     all_groups = request_groups.reshape(seq_count, DEVICE_REQUESTS)
     head_pages = lax.dynamic_index_in_dim(cache_pages, key_value_head, 1, keepdims=False)
+    page_part = head_pages.shape[1] // lax.axis_size("tc")
+    head_pages = lax.dynamic_slice_in_dim(head_pages, core_index * page_part, page_part, 1)
     outgoing = head_pages[held_slot[all_groups]]
     incoming = lax.all_to_all(outgoing, "seq", 0, 0, tiled=True)
+    both_parts = lax.all_gather(incoming, "tc", axis=0)
     page_source = holder[my_groups]
-    window_rows = incoming[page_source, lax.iota(jnp.int32, DEVICE_REQUESTS)[:, None]]
+    window_rows = both_parts[
+        lax.iota(jnp.int32, both_parts.shape[0])[None, None, :],
+        page_source[:, :, None],
+        lax.iota(jnp.int32, DEVICE_REQUESTS)[:, None, None],
+    ]
     window_rows = window_rows.reshape(DEVICE_REQUESTS, WINDOW_LENGTH, 2 * HEAD_SIZE)
     starts = jnp.cumsum(lengths) - lengths
     bounds = jnp.concatenate([starts, starts + lengths]).astype(jnp.int32)
@@ -96,12 +104,15 @@
         [query_rows, jnp.zeros_like(query_rows)], axis=-1
     ).transpose(1, 0, 2)
     attended = attend(bounds, query_pad, window_rows, fresh_pad)
-    gathered_heads = lax.all_gather(attended, "tensor", axis=0, tiled=True)
-    columns = out_weight.shape[1] // lax.axis_size("tensor")
+    along_z = lax.all_gather(attended, "tz", axis=0)
+    all_heads = lax.all_gather(along_z, "tc", axis=0)
+    columns = out_weight.shape[1] // (lax.axis_size("tz") * lax.axis_size("tc"))
     my_columns = lax.dynamic_slice_in_dim(out_weight, tensor_rank_index * columns, columns, 1)
-    my_columns = my_columns.reshape(gathered_heads.shape[0], HEAD_SIZE, columns)
+    my_columns = my_columns.reshape(
+        along_z.shape[0], all_heads.shape[0], resident_heads, HEAD_SIZE, columns
+    )
     projected = jnp.einsum(
-        "hrd,hdc->rc", gathered_heads, my_columns, preferred_element_type=jnp.float32
+        "czhrd,zchdn->rn", all_heads, my_columns, preferred_element_type=jnp.float32
     )
     return projected.astype(jnp.bfloat16)
 
@@ -191,13 +202,18 @@
 
 
 def solution(mesh):
+    cores = 2
+    seq_size, tensor_size = mesh.devices.shape
+    split_mesh = jax.sharding.Mesh(
+        mesh.devices.reshape(seq_size, tensor_size // cores, cores), ("seq", "tz", "tc")
+    )
     return jax.shard_map(
         body,
-        mesh=mesh,
+        mesh=split_mesh,
         in_specs=(
             P("seq", None),
             P(),
-            P(None, "tensor"),
+            P(None, ("tz", "tc")),
             P(),
             P(),
             P("seq", None, None, None),
@@ -205,6 +221,6 @@
             P(),
             P(),
         ),
-        out_specs=P("seq", "tensor"),
+        out_specs=P("seq", ("tz", "tc")),
         check_vma=False,
     )

time: 144 us -> 155 us (1.076)
  waiting for transfers between devices: 54.5 us -> 64.3 us
  Pallas kernels: 29.5 us -> 33.5 us
  local copies, waits for them, and re-layouts: 24.9 us -> 23.3 us
    all_gather x1 -> x3, waiting for transfers between devices: 31 us -> 46 us  [the longest x1 25.7 us: body(): along_z = lax.all_gather(attended, 'tz', axis=0)]
    all_to_all x1, waiting for transfers between devices: 23.5 us -> 18.2 us  [body(): incoming = lax.all_to_all(outgoing, 'seq', 0, 0, tiled=True)]
    pallas_call x1, Pallas kernels: 29.5 us -> 33.5 us  [attend(): pl.pallas_call(attend_kernel, out_shape=jax.ShapeDtypeStruct((heads, row_...]
    squeeze x1 -> x0, local copies, waits for them, and re-layouts: 3.2 us -> none  [body(): lax.dynamic_index_in_dim(cache_pages, key_value_head, 1, keepdims=False)]
    gather x3, local copies, waits for them, and re-layouts: 5.43 us -> 3.19 us  [body(): outgoing = head_pages[held_slot[all_groups]]]
    dynamic_slice x0 -> x1, local copies, waits for them, and re-layouts: none -> 1.66 us  [body(): lax.dynamic_slice_in_dim(head_pages, core_index * page_part, page_part, 1)]
    unnamed x16 -> x18, local copies, waits for them, and re-layouts: 2.74 us -> 3.79 us
  transfers between devices with their start and end apart: 2 -> 4, of which waited for: 2 -> 4; matrix products, arithmetic and copies ran while one was open for 9% -> 8% of each run, Pallas kernels for 0% -> 0%
where the time goes in v3:
time: 155 us; the launch traced here: 154 us
  waiting for transfers between devices  64.3 us (41%)
  Pallas kernels  33.5 us (22%)
  local copies, waits for them, and re-layouts  23.3 us (15%)
  between operations  13.3 us (9%)
  starting transfers between devices  7.83 us (5%)
  matrix products  7.28 us (5%)
  other arithmetic  5.08 us (3%)
    pallas_call x1, Pallas kernels, attend(): pl.pallas_call(attend_kernel, out_shape=jax.ShapeDtypeStruct((heads, row_...  33.5 us
    all_gather x1, waiting for transfers between devices, body(): along_z = lax.all_gather(attended, 'tz', axis=0)  25.7 us
    all_to_all x1, waiting for transfers between devices, body(): incoming = lax.all_to_all(outgoing, 'seq', 0, 0, tiled=True)  18.2 us
    all_gather x1, waiting for transfers between devices, body(): all_heads = lax.all_gather(along_z, 'tc', axis=0)  15.6 us
    all_to_all x1, starting transfers between devices, body(): incoming = lax.all_to_all(outgoing, 'seq', 0, 0, tiled=True)  7.7 us
    gather x1, local copies, waits for them, and re-layouts, body(): both_parts[lax.iota(jnp.int32, both_parts.shape[0])[None, None, :], page_...  5.76 us
    all_gather x1, waiting for transfers between devices, body(): both_parts = lax.all_gather(incoming, 'tc', axis=0)  4.69 us
    unnamed x18, local copies, waits for them, and re-layouts  3.79 us
  transfers between devices with their start and end apart: 4, of which 4 were waited for; matrix products, arithmetic and copies ran while one was open for 8% of the time, Pallas kernels for 0%

profile of v3, /device:TPU:1, one launch (start us, length us, event | category | flops | bytes accessed | tf_op | source)
XLA Modules:
  0.0 154.5 jit_solution(16808356211595704906)
XLA Ops:
  6.5 0.9 add_select_fusion.1
  7.5 0.7 reshape.109
  8.2 0.1 reshape.114
  8.3 0.9 fusion.15
  9.2 1.2 gather_fusion
  10.5 0.1 reshape.122
  10.7 1.7 %dynamic-slice_bitcast_fusion = bf16[64,64,128]{2,1,0:T(8,128)(2,1)S(1)} fusion(bf16[64,4,128,128]{3,2,1,0:T(8,128)(2,1)} %param.14, s32[]{:T(128)S(6)} %select_n.76, s32[]{:T(128)S(6)} %select_n.78), kind=kLoop, calls=%fused_computation.16 | loop fusion | bytes 2097160 | tf_op jit(solution)/shard_map/dynamic_slice | solution.py:89
  12.3 1.9 %gather_fusion.1 = bf16[80,64,128]{2,1,0:T(8,128)(2,1)} fusion(bf16[64,64,128]{2,1,0:T(8,128)(2,1)S(1)} %dynamic-slice_bitcast_fusion, s32[1024]{0:T(1024)S(1)} %pad_clamp_fusion.1), kind=kCustom, calls=%fused_computation.1 | custom fusion | bytes 2621760 | tf_op jit(solution)/shard_map/gather | solution.py:90
  14.2 7.7 %all-to-all-start = ((bf16[16,5,64,128]{3,2,1,0:T(8,128)(2,1)}), bf16[16,5,64,128]{3,2,1,0:T(8,128)(2,1)S(1)}, u32[]{:S(2)}, u32[]{:S(2)}) async-start(bf16[16,5,64,128]{3,2,1,0:T(8,128)(2,1)} %bitcast.34), calls=%async_computation | async-start | bytes 2621440 | tf_op jit(solution)/shard_map/all_to_all | solution.py:91
  22.0 18.2 %all-to-all-done = bf16[16,5,64,128]{3,2,1,0:T(8,128)(2,1)S(1)} async-done(((bf16[16,5,64,128]{3,2,1,0:T(8,128)(2,1)}), bf16[16,5,64,128]{3,2,1,0:T(8,128)(2,1)S(1)}, u32[]{:S(2)}, u32[]{:S(2)}) %all-to-all-start) | async-done | bytes 1310752 | tf_op jit(solution)/shard_map/all_to_all | solution.py:91
  40.2 1.1 copy-done.3
  41.3 0.1 compare_select_fusion.3
  41.4 0.6 gather_fusion.2
  42.1 0.1 reshape.136
  42.3 0.2 reduce-window.9
  42.5 2.7 %fusion = f32[768]{0:T(1024)S(1)} fusion(bf16[768,2048]{1,0:T(8,128)(2,1)} %param.9), kind=kLoop, calls=%fused_computation.6 | loop fusion | flops 4717824 | bytes 3148800 | tf_op jit(solution)/shard_map/reduce_sum | solution.py:24
  45.2 0.1 copy-done.4
  45.3 2.6 %convolution_convert_fusion = bf16[768,256]{0,1:T(8,128)(2,1)S(1)} fusion(bf16[2048,256]{1,0:T(8,128)(2,1)} %param.11, bf16[768,2048]{1,0:T(8,128)(2,1)S(1)} %copy-done.4, f32[2048]{0:T(1024)S(1)} %copy-done.8, f32[768]{0:T(1024)S(1)} %add_rsqrt_fusion), kind=kOutput, calls=%fused_computation.13 | convolution fusion | flops 811794432 | bytes 4598784 | tf_op jit(solution)/shard_map/dot_general | solution.py:68
  47.9 1.2 copy.15
  49.2 1.4 pad_bitcast_fusion.q_ref
  50.7 1.1 constant_dynamic-slice_fusion.1
  51.8 1.0 convolution_convert_fusion.1.fresh_ref
  52.9 4.7 %all-gather.7.cloned.1.call-done = bf16[32,5,64,128]{3,2,1,0:T(8,128)(2,1)} async-done(((bf16[16,5,64,128]{3,2,1,0:T(8,128)(2,1)}), bf16[32,5,64,128]{3,2,1,0:T(8,128)(2,1)}) %all-gather.7.cloned.1.call-update) | async-done | bytes 2621456 | tf_op jit(solution)/shard_map/all_gather | solution.py:92
  57.6 5.8 %gather_fusion.3 = bf16[160,64,128]{2,1,0:T(8,128)(2,1)} fusion(bf16[2,16,5,64,128]{4,3,2,1,0:T(8,128)(2,1)} %bitcast.35, s32[160]{0:T(256)S(1)} %reshape.136), kind=kCustom, calls=%fused_computation.3 | custom fusion | bytes 5244800 | tf_op jit(solution)/shard_map/gather | solution.py:94
  63.3 1.7 %copy-done.1 = bf16[160,64,128]{2,1,0:T(8,128)(2,1)S(1)} copy-done((bf16[160,64,128]{2,1,0:T(8,128)(2,1)S(1)}, bf16[160,64,128]{2,1,0:T(8,128)(2,1)}, u32[]{:S(2)}) %copy-start.1) | copy-done | bytes 2621464
  65.1 33.5 %shard_map.91 = bf16[4,768,64]{2,1,0:T(8,128)(2,1)S(1)} custom-call(s32[10]{0:T(128)S(1)} %pad_add_fusion.bounds_ref, bf16[4,768,128]{2,1,0:T(8,128)(2,1)S(1)} %pad_bitcast_fusion.q_ref, bf16[5,2048,128]{2,1,0:T(8,128)(2,1)S(1)} %bitcast.33, bf16[768,128]{1,0:T(8,128)(2,1)S(1)} %convolution_convert_fusion.1.fresh_ref), custom_call_target="tpu_custom_call" | custom-call | tf_op jit(solution)/shard_map/pallas_call | solution.py:185
  98.5 0.9 copy-done.2
  99.4 2.1 %copy.17 = bf16[4,768,64]{1,2,0:T(8,128)(2,1)} copy(bf16[4,768,64]{2,1,0:T(8,128)(2,1)} %copy-done.2) | data formatting | bytes 786432 | tf_op jit(solution)/shard_map/pallas_call | solution.py:185
  101.6 25.7 %all-gather.9.cloned.1.call-done = bf16[16,768,64]{1,2,0:T(8,128)(2,1)} async-done(((bf16[4,768,64]{1,2,0:T(8,128)(2,1)}), bf16[16,768,64]{1,2,0:T(8,128)(2,1)}) %all-gather.9.cloned.1.call-update) | async-done | bytes 1572880 | tf_op jit(solution)/shard_map/all_gather | solution.py:107
  127.4 1.3 constant_dynamic-slice_fusion
  128.7 15.6 %all-gather.11.cloned.1.call-done = bf16[8,4,768,64]{2,3,1,0:T(8,128)(2,1)} async-done(((bf16[4,4,768,64]{2,3,1,0:T(8,128)(2,1)}), bf16[8,4,768,64]{2,3,1,0:T(8,128)(2,1)}) %all-gather.11.cloned.1.call-update) | async-done | bytes 3145744 | tf_op jit(solution)/shard_map/all_gather | solution.py:108
  144.3 3.7 %fusion.8 = bf16[768,256]{1,0:T(8,128)(2,1)} fusion(bf16[2,4,4,768,64]{3,4,2,1,0:T(8,128)(2,1)} %bitcast.40, bf16[4,2,4,64,256]{4,3,2,1,0:T(8,128)(2,1)S(1)} %bitcast.37), kind=kOutput, calls=%fused_computation.12 | convolution fusion | flops 805502976 | bytes 4587520 | tf_op jit(solution)/shard_map/czhrd,zchdn->rn/dot_general | solution.py:114
  (32 shorter events, 0.6 us)
Async XLA Ops:
  6.5 44.1 %copy-start = (bf16[2048,4,128]{2,1,0:T(4,128)(2,1)S(1)}, bf16[2048,4,128]{2,1,0:T(4,128)(2,1)}, u32[]{:S(2)}) copy-start(bf16[2048,4,128]{2,1,0:T(4,128)(2,1)} %param.12) | copy-start | bytes 6291460
  12.3 29.0 %copy-start.6 = (s32[80]{0:T(128)S(1)}, s32[80]{0:T(128)}, u32[]{:S(2)}) copy-start(s32[80]{0:T(128)} %param.17) | copy-start | bytes 964
  12.3 29.9 %copy-start.7 = (s32[80]{0:T(128)S(1)}, s32[80]{0:T(128)}, u32[]{:S(2)}) copy-start(s32[80]{0:T(128)} %param.16) | copy-start | bytes 964
  14.2 31.0 %copy-start.8 = (f32[2048]{0:T(1024)S(1)}, f32[2048]{0:T(1024)}, u32[]{:S(2)}) copy-start(f32[2048]{0:T(1024)} %param.10) | copy-start | bytes 24580
  14.2 26.0 %all-to-all-start = ((bf16[16,5,64,128]{3,2,1,0:T(8,128)(2,1)}), bf16[16,5,64,128]{3,2,1,0:T(8,128)(2,1)S(1)}, u32[]{:S(2)}, u32[]{:S(2)}) async-start(bf16[16,5,64,128]{3,2,1,0:T(8,128)(2,1)} %bitcast.34), calls=%async_computation | async-start | bytes 2621440 | tf_op jit(solution)/shard_map/all_to_all | solution.py:91
  21.9 35.6 %all-gather.7.cloned.1.call-start = ((), (), s32[]{:S(2)}) async-start(), calls=%async_computation.1 | async-start | bytes 3932160 | tf_op jit(solution)/shard_map/all_gather | solution.py:92
  40.2 1.1 copy-start.3
  41.3 86.1 %all-gather.9.cloned.1.call-start = ((), (), s32[]{:S(2)}) async-start(), calls=%async_computation.2 | async-start | bytes 1966080 | tf_op jit(solution)/shard_map/all_gather | solution.py:107
  42.5 2.8 %copy-start.4 = (bf16[768,2048]{1,0:T(8,128)(2,1)S(1)}, bf16[768,2048]{1,0:T(8,128)(2,1)}, u32[]{:S(2)}) copy-start(bf16[768,2048]{1,0:T(8,128)(2,1)} %param.9) | copy-start | bytes 9437188
  49.1 2.8 %copy-start.5 = (bf16[768,2048]{1,0:T(8,128)(2,1)S(1)}, bf16[768,2048]{1,0:T(8,128)(2,1)}, u32[]{:S(2)}) copy-start(bf16[768,2048]{1,0:T(8,128)(2,1)} %param.9) | copy-start | bytes 9437188
  63.3 1.7 %copy-start.1 = (bf16[160,64,128]{2,1,0:T(8,128)(2,1)S(1)}, bf16[160,64,128]{2,1,0:T(8,128)(2,1)}, u32[]{:S(2)}) copy-start(bf16[160,64,128]{2,1,0:T(8,128)(2,1)} %gather_fusion.3) | copy-start | bytes 7864324
  98.5 0.9 copy-start.2
  101.6 42.7 %all-gather.11.cloned.1.call-start = ((), (), s32[]{:S(2)}) async-start(), calls=%async_computation.3 | async-start | bytes 4718592 | tf_op jit(solution)/shard_map/all_gather | solution.py:108
Sparse Core Ops, SparseCore 0:
  41.4 16.1 all-gather.6
  101.7 25.6 all-gather.8
  129.0 15.2 all-gather.10

commit v4 on v3

--- a/solution.py
+++ b/solution.py
@@ -104,16 +104,10 @@
         [query_rows, jnp.zeros_like(query_rows)], axis=-1
     ).transpose(1, 0, 2)
     attended = attend(bounds, query_pad, window_rows, fresh_pad)
-    along_z = lax.all_gather(attended, "tz", axis=0)
-    all_heads = lax.all_gather(along_z, "tc", axis=0)
+    all_heads = lax.all_gather(attended, ("tz", "tc"), axis=1, tiled=True)
     columns = out_weight.shape[1] // (lax.axis_size("tz") * lax.axis_size("tc"))
     my_columns = lax.dynamic_slice_in_dim(out_weight, tensor_rank_index * columns, columns, 1)
-    my_columns = my_columns.reshape(
-        along_z.shape[0], all_heads.shape[0], resident_heads, HEAD_SIZE, columns
-    )
-    projected = jnp.einsum(
-        "czhrd,zchdn->rn", all_heads, my_columns, preferred_element_type=jnp.float32
-    )
+    projected = jnp.dot(all_heads, my_columns, preferred_element_type=jnp.float32)
     return projected.astype(jnp.bfloat16)
 
 
@@ -175,7 +169,9 @@
     out_acc = lax.fori_loop(
         r_first, r_last + 1, one_request, jnp.zeros((stacked, 2 * HEAD_SIZE), jnp.float32)
     )
-    o_ref[...] = out_acc[:, HEAD_SIZE:].astype(o_ref.dtype).reshape(heads, block_rows, HEAD_SIZE)
+    result = out_acc[:, HEAD_SIZE:].astype(o_ref.dtype)
+    for h in range(heads):
+        o_ref[:, h * HEAD_SIZE : (h + 1) * HEAD_SIZE] = result[h * block_rows : (h + 1) * block_rows]
 
 
 def attend(bounds, query_pad, window_rows, fresh_rows):
@@ -184,7 +180,7 @@
     requests, window, _ = window_rows.shape
     return pl.pallas_call(
         attend_kernel,
-        out_shape=jax.ShapeDtypeStruct((heads, row_count, HEAD_SIZE), jnp.bfloat16),
+        out_shape=jax.ShapeDtypeStruct((row_count, heads * HEAD_SIZE), jnp.bfloat16),
         grid_spec=pltpu.PrefetchScalarGridSpec(
             num_scalar_prefetch=1,
             grid=(row_count // block_rows,),
@@ -193,7 +189,7 @@
                 pl.BlockSpec((requests, window, width), lambda i, b: (0, 0, 0)),
                 pl.BlockSpec((row_count, width), lambda i, b: (0, 0)),
             ],
-            out_specs=pl.BlockSpec((heads, block_rows, HEAD_SIZE), lambda i, b: (0, i, 0)),
+            out_specs=pl.BlockSpec((block_rows, heads * HEAD_SIZE), lambda i, b: (i, 0)),
         ),
         compiler_params=pltpu.CompilerParams(
             dimension_semantics=("arbitrary",), vmem_limit_bytes=48 * 1024 * 1024

time: 155 us -> 143 us (0.923)
  waiting for transfers between devices: 64.3 us -> 59.1 us
  local copies, waits for them, and re-layouts: 23.3 us -> 19 us
  Pallas kernels: 33.5 us -> 30.4 us
    all_gather x2 -> x1, waiting for transfers between devices: 41.3 us -> 36.2 us  [body(): all_heads = lax.all_gather(attended, ('tz', 'tc'), axis=1, tiled=True)]
    pallas_call x1, Pallas kernels: 33.5 us -> 30.4 us  [attend(): pl.pallas_call(attend_kernel, out_shape=jax.ShapeDtypeStruct((row_count,...]
    pallas_call x1 -> x0, local copies, waits for them, and re-layouts: 2.13 us -> none  [attend(): pl.pallas_call(attend_kernel, out_shape=jax.ShapeDtypeStruct((heads, row_...]
    unnamed x18 -> x16, local copies, waits for them, and re-layouts: 3.79 us -> 2.92 us
  transfers between devices with their start and end apart: 4 -> 3, of which waited for: 4 -> 3; matrix products, arithmetic and copies ran while one was open for 8% -> 8% of each run, Pallas kernels for 0% -> 0%
where the time goes in v4:
time: 143 us; the launch traced here: 142 us
  waiting for transfers between devices  59.1 us (41%)
  Pallas kernels  30.4 us (21%)
  local copies, waits for them, and re-layouts  19 us (13%)
  between operations  13.6 us (10%)
  starting transfers between devices  7.78 us (5%)
  matrix products  7.51 us (5%)
  other arithmetic  5.08 us (4%)
    all_gather x1, waiting for transfers between devices, body(): all_heads = lax.all_gather(attended, ('tz', 'tc'), axis=1, tiled=True)  36.2 us
    pallas_call x1, Pallas kernels, attend(): pl.pallas_call(attend_kernel, out_shape=jax.ShapeDtypeStruct((row_count,...  30.4 us
    all_to_all x1, waiting for transfers between devices, body(): incoming = lax.all_to_all(outgoing, 'seq', 0, 0, tiled=True)  18.2 us
    all_to_all x1, starting transfers between devices, body(): incoming = lax.all_to_all(outgoing, 'seq', 0, 0, tiled=True)  7.7 us
    gather x1, local copies, waits for them, and re-layouts, body(): both_parts[lax.iota(jnp.int32, both_parts.shape[0])[None, None, :], page_...  5.75 us
    all_gather x1, waiting for transfers between devices, body(): both_parts = lax.all_gather(incoming, 'tc', axis=0)  4.66 us
    dot_general x1, matrix products, body(): jnp.dot(all_heads, my_columns, preferred_element_type=jnp.float32)  3.9 us
    gather x3, local copies, waits for them, and re-layouts, body(): outgoing = head_pages[held_slot[all_groups]]  3.17 us
  transfers between devices with their start and end apart: 3, of which 3 were waited for; matrix products, arithmetic and copies ran while one was open for 8% of the time, Pallas kernels for 0%

profile of v4, /device:TPU:1, one launch (start us, length us, event | category | flops | bytes accessed | tf_op | source)
XLA Modules:
  0.0 142.5 jit_solution(15126461426692435975)
XLA Ops:
  6.5 0.9 add_select_fusion.1
  7.5 0.7 reshape.106
  8.2 0.1 reshape.110
  8.3 0.9 fusion.7
  9.2 1.2 gather_fusion
  10.5 0.1 gather.15
  10.5 0.1 reshape.118
  10.7 1.7 %dynamic-slice_bitcast_fusion = bf16[64,64,128]{2,1,0:T(8,128)(2,1)S(1)} fusion(bf16[64,4,128,128]{3,2,1,0:T(8,128)(2,1)} %param.14, s32[]{:T(128)S(6)} %select_n.76, s32[]{:T(128)S(6)} %select_n.78), kind=kLoop, calls=%fused_computation.13 | loop fusion | bytes 2097160 | tf_op jit(solution)/shard_map/dynamic_slice | solution.py:89
  12.3 1.9 %gather_fusion.1 = bf16[80,64,128]{2,1,0:T(8,128)(2,1)} fusion(bf16[64,64,128]{2,1,0:T(8,128)(2,1)S(1)} %dynamic-slice_bitcast_fusion, s32[1024]{0:T(1024)S(1)} %pad_clamp_fusion.1), kind=kCustom, calls=%fused_computation.1 | custom fusion | bytes 2621760 | tf_op jit(solution)/shard_map/gather | solution.py:90
  14.2 7.7 %all-to-all-start = ((bf16[16,5,64,128]{3,2,1,0:T(8,128)(2,1)}), bf16[16,5,64,128]{3,2,1,0:T(8,128)(2,1)S(1)}, u32[]{:S(2)}, u32[]{:S(2)}) async-start(bf16[16,5,64,128]{3,2,1,0:T(8,128)(2,1)} %bitcast.26), calls=%async_computation | async-start | bytes 2621440 | tf_op jit(solution)/shard_map/all_to_all | solution.py:91
  22.0 18.2 %all-to-all-done = bf16[16,5,64,128]{3,2,1,0:T(8,128)(2,1)S(1)} async-done(((bf16[16,5,64,128]{3,2,1,0:T(8,128)(2,1)}), bf16[16,5,64,128]{3,2,1,0:T(8,128)(2,1)S(1)}, u32[]{:S(2)}, u32[]{:S(2)}) %all-to-all-start) | async-done | bytes 1310752 | tf_op jit(solution)/shard_map/all_to_all | solution.py:91
  40.2 1.1 copy-done.2
  41.3 0.1 compare_select_fusion.3
  41.4 0.6 gather_fusion.2
  42.0 0.1 shift-left_or_fusion
  42.1 0.1 reshape.132
  42.2 0.1 dynamic-slice_bitcast_fusion.1
  42.3 0.2 reduce-window.9
  42.5 2.7 %fusion = f32[768]{0:T(1024)S(1)} fusion(bf16[768,2048]{1,0:T(8,128)(2,1)} %param.9), kind=kLoop, calls=%fused_computation.6 | loop fusion | flops 4717824 | bytes 3148800 | tf_op jit(solution)/shard_map/reduce_sum | solution.py:24
  45.2 0.1 copy-done.3
  45.3 2.6 %convolution_convert_fusion.1 = bf16[768,256]{0,1:T(8,128)(2,1)S(1)} fusion(bf16[2048,256]{1,0:T(8,128)(2,1)} %param.11, bf16[768,2048]{1,0:T(8,128)(2,1)S(1)} %copy-done.3, f32[2048]{0:T(1024)S(1)} %copy-done.7, f32[768]{0:T(1024)S(1)} %add_rsqrt_fusion), kind=kOutput, calls=%fused_computation.10 | convolution fusion | flops 811794432 | bytes 4598784 | tf_op jit(solution)/shard_map/dot_general | solution.py:68
  47.9 1.2 copy.12
  49.2 0.1 pad_add_fusion.bounds_ref
  49.2 1.4 %pad_bitcast_fusion.q_ref = bf16[4,768,128]{2,1,0:T(8,128)(2,1)S(1)} fusion(bf16[768,4,64]{2,0,1:T(8,128)(2,1)} %copy.12), kind=kLoop, calls=%fused_computation.14 | loop fusion | bytes 1179648 | tf_op jit(solution)/shard_map/transpose | solution.py:105
  50.7 1.1 constant_dynamic-slice_fusion
  51.8 1.0 convolution_convert_fusion.2.fresh_ref
  52.9 4.7 %all-gather.6.cloned.1.call-done = bf16[32,5,64,128]{3,2,1,0:T(8,128)(2,1)} async-done(((bf16[16,5,64,128]{3,2,1,0:T(8,128)(2,1)}), bf16[32,5,64,128]{3,2,1,0:T(8,128)(2,1)}) %all-gather.6.cloned.1.call-update) | async-done | bytes 2621456 | tf_op jit(solution)/shard_map/all_gather | solution.py:92
  57.6 5.7 %gather_fusion.3 = bf16[160,64,128]{2,1,0:T(8,128)(2,1)} fusion(bf16[2,16,5,64,128]{4,3,2,1,0:T(8,128)(2,1)} %bitcast.27, s32[160]{0:T(256)S(1)} %reshape.132), kind=kCustom, calls=%fused_computation.3 | custom fusion | bytes 5244800 | tf_op jit(solution)/shard_map/gather | solution.py:94
  63.3 1.7 %copy-done.1 = bf16[160,64,128]{2,1,0:T(8,128)(2,1)S(1)} copy-done((bf16[160,64,128]{2,1,0:T(8,128)(2,1)S(1)}, bf16[160,64,128]{2,1,0:T(8,128)(2,1)}, u32[]{:S(2)}) %copy-start.1) | copy-done | bytes 2621464
  65.0 30.4 %shard_map.91 = bf16[768,256]{1,0:T(8,128)(2,1)} custom-call(s32[10]{0:T(128)S(1)} %pad_add_fusion.bounds_ref, bf16[4,768,128]{2,1,0:T(8,128)(2,1)S(1)} %pad_bitcast_fusion.q_ref, bf16[5,2048,128]{2,1,0:T(8,128)(2,1)S(1)} %bitcast.25, bf16[768,128]{1,0:T(8,128)(2,1)S(1)} %convolution_convert_fusion.2.fresh_ref), custom_call_target="tpu_custom_call" | custom-call | tf_op jit(solution)/shard_map/pallas_call | solution.py:181
  95.5 36.2 %all-gather.4.cloned.1.call-done = bf16[768,2048]{1,0:T(8,128)(2,1)} async-done(((bf16[768,256]{1,0:T(8,128)(2,1)}), bf16[768,2048]{1,0:T(8,128)(2,1)}) %all-gather.4.cloned.1.call-update) | async-done | bytes 3145744 | tf_op jit(solution)/shard_map/all_gather | solution.py:107
  131.7 3.9 %convolution_convert_fusion = bf16[768,256]{1,0:T(8,128)(2,1)} fusion(bf16[768,2048]{1,0:T(8,128)(2,1)} %all-gather.4.cloned.1.call-done, bf16[2048,2048]{1,0:T(8,128)(2,1)} %param.13, s32[]{:T(128)S(6)} %select_n.86), kind=kOutput, calls=%fused_computation.9 | convolution fusion | flops 805502976 | bytes 4587524 | tf_op jit(solution)/shard_map/dot_general | solution.py:110
  (25 shorter events, 0.3 us)
Async XLA Ops:
  6.5 44.1 %copy-start = (bf16[2048,4,128]{2,1,0:T(4,128)(2,1)S(1)}, bf16[2048,4,128]{2,1,0:T(4,128)(2,1)}, u32[]{:S(2)}) copy-start(bf16[2048,4,128]{2,1,0:T(4,128)(2,1)} %param.12) | copy-start | bytes 6291460
  12.3 29.0 %copy-start.5 = (s32[80]{0:T(128)S(1)}, s32[80]{0:T(128)}, u32[]{:S(2)}) copy-start(s32[80]{0:T(128)} %param.17) | copy-start | bytes 964
  12.3 29.9 %copy-start.6 = (s32[80]{0:T(128)S(1)}, s32[80]{0:T(128)}, u32[]{:S(2)}) copy-start(s32[80]{0:T(128)} %param.16) | copy-start | bytes 964
  14.2 31.0 %copy-start.7 = (f32[2048]{0:T(1024)S(1)}, f32[2048]{0:T(1024)}, u32[]{:S(2)}) copy-start(f32[2048]{0:T(1024)} %param.10) | copy-start | bytes 24580
  14.2 26.0 %all-to-all-start = ((bf16[16,5,64,128]{3,2,1,0:T(8,128)(2,1)}), bf16[16,5,64,128]{3,2,1,0:T(8,128)(2,1)S(1)}, u32[]{:S(2)}, u32[]{:S(2)}) async-start(bf16[16,5,64,128]{3,2,1,0:T(8,128)(2,1)} %bitcast.26), calls=%async_computation | async-start | bytes 2621440 | tf_op jit(solution)/shard_map/all_to_all | solution.py:91
  21.9 35.6 %all-gather.6.cloned.1.call-start = ((), (), s32[]{:S(2)}) async-start(), calls=%async_computation.2 | async-start | bytes 3932160 | tf_op jit(solution)/shard_map/all_gather | solution.py:92
  40.2 1.1 copy-start.2
  41.3 90.4 %all-gather.4.cloned.1.call-start = ((), (), s32[]{:S(2)}) async-start(), calls=%async_computation.1 | async-start | bytes 3538944 | tf_op jit(solution)/shard_map/all_gather | solution.py:107
  42.5 2.8 %copy-start.3 = (bf16[768,2048]{1,0:T(8,128)(2,1)S(1)}, bf16[768,2048]{1,0:T(8,128)(2,1)}, u32[]{:S(2)}) copy-start(bf16[768,2048]{1,0:T(8,128)(2,1)} %param.9) | copy-start | bytes 9437188
  49.1 2.8 %copy-start.4 = (bf16[768,2048]{1,0:T(8,128)(2,1)S(1)}, bf16[768,2048]{1,0:T(8,128)(2,1)}, u32[]{:S(2)}) copy-start(bf16[768,2048]{1,0:T(8,128)(2,1)} %param.9) | copy-start | bytes 9437188
  63.3 1.7 %copy-start.1 = (bf16[160,64,128]{2,1,0:T(8,128)(2,1)S(1)}, bf16[160,64,128]{2,1,0:T(8,128)(2,1)}, u32[]{:S(2)}) copy-start(bf16[160,64,128]{2,1,0:T(8,128)(2,1)} %gather_fusion.3) | copy-start | bytes 7864324
Sparse Core Ops, SparseCore 0:
  41.4 16.1 all-gather.5
  95.6 36.0 all-gather.3

commit v5 on v4

--- a/solution.py
+++ b/solution.py
@@ -104,10 +104,17 @@
         [query_rows, jnp.zeros_like(query_rows)], axis=-1
     ).transpose(1, 0, 2)
     attended = attend(bounds, query_pad, window_rows, fresh_pad)
-    all_heads = lax.all_gather(attended, ("tz", "tc"), axis=1, tiled=True)
-    columns = out_weight.shape[1] // (lax.axis_size("tz") * lax.axis_size("tc"))
+    along_z = lax.all_gather(attended, "tz", axis=1, tiled=True)
+    all_heads = lax.all_gather(along_z, "tc", axis=1)
+    z_count = lax.axis_size("tz")
+    core_count = lax.axis_size("tc")
+    columns = out_weight.shape[1] // (z_count * core_count)
     my_columns = lax.dynamic_slice_in_dim(out_weight, tensor_rank_index * columns, columns, 1)
-    projected = jnp.dot(all_heads, my_columns, preferred_element_type=jnp.float32)
+    my_columns = my_columns.reshape(z_count, core_count, attended.shape[1], columns)
+    all_heads = all_heads.reshape(row_count, core_count, z_count, attended.shape[1])
+    projected = jnp.einsum(
+        "rczj,zcjn->rn", all_heads, my_columns, preferred_element_type=jnp.float32
+    )
     return projected.astype(jnp.bfloat16)
 
 

time: 143 us -> 163 us (1.14)
  waiting for transfers between devices: 59.1 us -> 78.7 us
  local copies, waits for them, and re-layouts: 19 us -> 26.5 us
  Pallas kernels: 30.4 us -> 23.6 us
    all_gather x1 -> x2, waiting for transfers between devices: 36.2 us -> 55.7 us  [the longest x1 38 us: body(): along_z = lax.all_gather(attended, 'tz', axis=1, tiled=True)]
    pallas_call x1, Pallas kernels: 30.4 us -> 23.6 us  [attend(): pl.pallas_call(attend_kernel, out_shape=jax.ShapeDtypeStruct((row_count,...]
    reshape x0 -> x1, local copies, waits for them, and re-layouts: none -> 6.16 us  [body(): all_heads.reshape(row_count, core_count, z_count, attended.shape[1])]
  transfers between devices with their start and end apart: 3 -> 4, of which waited for: 3 -> 4; matrix products, arithmetic and copies ran while one was open for 8% -> 8% of each run, Pallas kernels for 0% -> 0%
where the time goes in v5:
time: 163 us; the launch traced here: 162 us
  waiting for transfers between devices  78.7 us (48%)
  local copies, waits for them, and re-layouts  26.5 us (16%)
  Pallas kernels  23.6 us (14%)
  between operations  13.3 us (8%)
  starting transfers between devices  7.82 us (5%)
  matrix products  7.3 us (4%)
  other arithmetic  4.93 us (3%)
    all_gather x1, waiting for transfers between devices, body(): along_z = lax.all_gather(attended, 'tz', axis=1, tiled=True)  38 us
    pallas_call x1, Pallas kernels, attend(): pl.pallas_call(attend_kernel, out_shape=jax.ShapeDtypeStruct((row_count,...  23.6 us
    all_to_all x1, waiting for transfers between devices, body(): incoming = lax.all_to_all(outgoing, 'seq', 0, 0, tiled=True)  18.2 us
    all_gather x1, waiting for transfers between devices, body(): all_heads = lax.all_gather(along_z, 'tc', axis=1)  17.8 us
    all_to_all x1, starting transfers between devices, body(): incoming = lax.all_to_all(outgoing, 'seq', 0, 0, tiled=True)  7.7 us
    reshape x1, local copies, waits for them, and re-layouts, body(): all_heads.reshape(row_count, core_count, z_count, attended.shape[1])  6.16 us
    gather x1, local copies, waits for them, and re-layouts, body(): both_parts[lax.iota(jnp.int32, both_parts.shape[0])[None, None, :], page_...  5.75 us
    all_gather x1, waiting for transfers between devices, body(): both_parts = lax.all_gather(incoming, 'tc', axis=0)  4.7 us
  transfers between devices with their start and end apart: 4, of which 4 were waited for; matrix products, arithmetic and copies ran while one was open for 8% of the time, Pallas kernels for 0%

profile of v5, /device:TPU:1, one launch (start us, length us, event | category | flops | bytes accessed | tf_op | source)
XLA Modules:
  0.0 162.2 jit_solution(16314275120688847533)
XLA Ops:
  6.5 0.9 reshape.112
  7.4 0.1 reshape.118
  7.5 0.8 add_select_fusion.1
  8.3 0.9 fusion.15
  9.2 1.2 gather_fusion
  10.5 0.1 gather.15
  10.5 0.1 reshape.126
  10.7 1.7 %dynamic-slice_bitcast_fusion = bf16[64,64,128]{2,1,0:T(8,128)(2,1)S(1)} fusion(bf16[64,4,128,128]{3,2,1,0:T(8,128)(2,1)} %param.14, s32[]{:T(128)S(6)} %select_n.76, s32[]{:T(128)S(6)} %select_n.78), kind=kLoop, calls=%fused_computation.16 | loop fusion | bytes 2097160 | tf_op jit(solution)/shard_map/dynamic_slice | solution.py:89
  12.3 1.9 %gather_fusion.1 = bf16[80,64,128]{2,1,0:T(8,128)(2,1)} fusion(bf16[64,64,128]{2,1,0:T(8,128)(2,1)S(1)} %dynamic-slice_bitcast_fusion, s32[1024]{0:T(1024)S(1)} %pad_clamp_fusion.1), kind=kCustom, calls=%fused_computation.1 | custom fusion | bytes 2621760 | tf_op jit(solution)/shard_map/gather | solution.py:90
  14.2 7.7 %all-to-all-start = ((bf16[16,5,64,128]{3,2,1,0:T(8,128)(2,1)}), bf16[16,5,64,128]{3,2,1,0:T(8,128)(2,1)S(1)}, u32[]{:S(2)}, u32[]{:S(2)}) async-start(bf16[16,5,64,128]{3,2,1,0:T(8,128)(2,1)} %bitcast.32), calls=%async_computation | async-start | bytes 2621440 | tf_op jit(solution)/shard_map/all_to_all | solution.py:91
  22.0 18.2 %all-to-all-done = bf16[16,5,64,128]{3,2,1,0:T(8,128)(2,1)S(1)} async-done(((bf16[16,5,64,128]{3,2,1,0:T(8,128)(2,1)}), bf16[16,5,64,128]{3,2,1,0:T(8,128)(2,1)S(1)}, u32[]{:S(2)}, u32[]{:S(2)}) %all-to-all-start) | async-done | bytes 1310752 | tf_op jit(solution)/shard_map/all_to_all | solution.py:91
  40.2 1.1 copy-done.2
  41.3 0.1 dynamic-slice_bitcast_fusion.1
  41.4 0.2 reduce-window.9
  41.7 0.6 gather_fusion.2
  42.3 0.1 reshape.140
  42.5 2.7 %fusion = f32[768]{0:T(1024)S(1)} fusion(bf16[768,2048]{1,0:T(8,128)(2,1)} %param.9), kind=kLoop, calls=%fused_computation.6 | loop fusion | flops 4717824 | bytes 3148800 | tf_op jit(solution)/shard_map/reduce_sum | solution.py:24
  45.2 0.1 copy-done.3
  45.3 2.6 %convolution_convert_fusion = bf16[768,256]{0,1:T(8,128)(2,1)S(1)} fusion(bf16[2048,256]{1,0:T(8,128)(2,1)} %param.11, bf16[768,2048]{1,0:T(8,128)(2,1)S(1)} %copy-done.3, f32[2048]{0:T(1024)S(1)} %copy-done.7, f32[768]{0:T(1024)S(1)} %add_rsqrt_fusion), kind=kOutput, calls=%fused_computation.13 | convolution fusion | flops 811794432 | bytes 4598784 | tf_op jit(solution)/shard_map/dot_general | solution.py:68
  47.9 1.2 copy.15
  49.2 1.4 pad_bitcast_fusion.q_ref
  50.7 1.1 constant_dynamic-slice_fusion.1
  51.8 1.0 convolution_convert_fusion.1.fresh_ref
  52.9 4.7 %all-gather.8.cloned.1.call-done = bf16[32,5,64,128]{3,2,1,0:T(8,128)(2,1)} async-done(((bf16[16,5,64,128]{3,2,1,0:T(8,128)(2,1)}), bf16[32,5,64,128]{3,2,1,0:T(8,128)(2,1)}) %all-gather.8.cloned.1.call-update) | async-done | bytes 2621456 | tf_op jit(solution)/shard_map/all_gather | solution.py:92
  57.6 5.7 %gather_fusion.3 = bf16[160,64,128]{2,1,0:T(8,128)(2,1)} fusion(bf16[2,16,5,64,128]{4,3,2,1,0:T(8,128)(2,1)} %bitcast.33, s32[160]{0:T(256)S(1)} %reshape.140), kind=kCustom, calls=%fused_computation.3 | custom fusion | bytes 5244800 | tf_op jit(solution)/shard_map/gather | solution.py:94
  63.3 1.7 %copy-done.1 = bf16[160,64,128]{2,1,0:T(8,128)(2,1)S(1)} copy-done((bf16[160,64,128]{2,1,0:T(8,128)(2,1)S(1)}, bf16[160,64,128]{2,1,0:T(8,128)(2,1)}, u32[]{:S(2)}) %copy-start.1) | copy-done | bytes 2621464
  65.1 23.6 %shard_map.91 = bf16[768,256]{1,0:T(8,128)(2,1)} custom-call(s32[10]{0:T(128)S(1)} %pad_add_fusion.bounds_ref, bf16[4,768,128]{2,1,0:T(8,128)(2,1)S(1)} %pad_bitcast_fusion.q_ref, bf16[5,2048,128]{2,1,0:T(8,128)(2,1)S(1)} %bitcast.31, bf16[768,128]{1,0:T(8,128)(2,1)S(1)} %convolution_convert_fusion.1.fresh_ref), custom_call_target="tpu_custom_call" | custom-call | tf_op jit(solution)/shard_map/pallas_call | solution.py:188
  88.7 38.0 %all-gather.6.cloned.1.call-done = bf16[768,1024]{1,0:T(8,128)(2,1)} async-done(((bf16[768,256]{1,0:T(8,128)(2,1)}), bf16[768,1024]{1,0:T(8,128)(2,1)}) %all-gather.6.cloned.1.call-update) | async-done | bytes 1572880 | tf_op jit(solution)/shard_map/all_gather | solution.py:107
  126.7 1.3 constant_dynamic-slice_fusion
  128.0 17.8 %all-gather.10.cloned.1.call-done = bf16[768,2048]{1,0:T(8,128)(2,1)} async-done(((bf16[768,1024]{1,0:T(8,128)(2,1)}), bf16[768,2048]{1,0:T(8,128)(2,1)}) %all-gather.10.cloned.1.call-update) | async-done | bytes 3145744 | tf_op jit(solution)/shard_map/all_gather | solution.py:108
  145.8 6.2 %reshape.114 = bf16[768,2,4,256]{3,2,1,0:T(4,128)(2,1)} reshape(bf16[768,2048]{1,0:T(8,128)(2,1)} %all-gather.10.cloned.1.call-done) | data formatting | bytes 6291456 | tf_op jit(solution)/shard_map/reshape | solution.py:114
  152.0 3.7 %fusion.8 = bf16[768,256]{1,0:T(8,128)(2,1)} fusion(bf16[768,2,4,256]{3,2,1,0:T(4,128)(2,1)} %reshape.114, bf16[4,2,256,256]{3,2,1,0:T(8,128)(2,1)S(1)} %bitcast.34), kind=kOutput, calls=%fused_computation.12 | convolution fusion | flops 805502976 | bytes 4587520 | tf_op jit(solution)/shard_map/rczj,zcjn->rn/dot_general | solution.py:115
  (30 shorter events, 0.6 us)
Async XLA Ops:
  6.5 44.1 %copy-start = (bf16[2048,4,128]{2,1,0:T(4,128)(2,1)S(1)}, bf16[2048,4,128]{2,1,0:T(4,128)(2,1)}, u32[]{:S(2)}) copy-start(bf16[2048,4,128]{2,1,0:T(4,128)(2,1)} %param.12) | copy-start | bytes 6291460
  12.3 29.0 %copy-start.6 = (s32[80]{0:T(128)S(1)}, s32[80]{0:T(128)}, u32[]{:S(2)}) copy-start(s32[80]{0:T(128)} %param.16) | copy-start | bytes 964
  12.3 29.3 %copy-start.5 = (s32[80]{0:T(128)S(1)}, s32[80]{0:T(128)}, u32[]{:S(2)}) copy-start(s32[80]{0:T(128)} %param.17) | copy-start | bytes 964
  14.2 31.0 %copy-start.7 = (f32[2048]{0:T(1024)S(1)}, f32[2048]{0:T(1024)}, u32[]{:S(2)}) copy-start(f32[2048]{0:T(1024)} %param.10) | copy-start | bytes 24580
  14.2 26.0 %all-to-all-start = ((bf16[16,5,64,128]{3,2,1,0:T(8,128)(2,1)}), bf16[16,5,64,128]{3,2,1,0:T(8,128)(2,1)S(1)}, u32[]{:S(2)}, u32[]{:S(2)}) async-start(bf16[16,5,64,128]{3,2,1,0:T(8,128)(2,1)} %bitcast.32), calls=%async_computation | async-start | bytes 2621440 | tf_op jit(solution)/shard_map/all_to_all | solution.py:91
  21.9 35.6 %all-gather.8.cloned.1.call-start = ((), (), s32[]{:S(2)}) async-start(), calls=%async_computation.2 | async-start | bytes 3932160 | tf_op jit(solution)/shard_map/all_gather | solution.py:92
  40.2 1.1 copy-start.2
  41.3 85.4 %all-gather.6.cloned.1.call-start = ((), (), s32[]{:S(2)}) async-start(), calls=%async_computation.1 | async-start | bytes 1966080 | tf_op jit(solution)/shard_map/all_gather | solution.py:107
  42.5 2.8 %copy-start.3 = (bf16[768,2048]{1,0:T(8,128)(2,1)S(1)}, bf16[768,2048]{1,0:T(8,128)(2,1)}, u32[]{:S(2)}) copy-start(bf16[768,2048]{1,0:T(8,128)(2,1)} %param.9) | copy-start | bytes 9437188
  49.1 2.8 %copy-start.4 = (bf16[768,2048]{1,0:T(8,128)(2,1)S(1)}, bf16[768,2048]{1,0:T(8,128)(2,1)}, u32[]{:S(2)}) copy-start(bf16[768,2048]{1,0:T(8,128)(2,1)} %param.9) | copy-start | bytes 9437188
  63.3 1.7 %copy-start.1 = (bf16[160,64,128]{2,1,0:T(8,128)(2,1)S(1)}, bf16[160,64,128]{2,1,0:T(8,128)(2,1)}, u32[]{:S(2)}) copy-start(bf16[160,64,128]{2,1,0:T(8,128)(2,1)} %gather_fusion.3) | copy-start | bytes 7864324
  88.7 57.1 %all-gather.10.cloned.1.call-start = ((), (), s32[]{:S(2)}) async-start(), calls=%async_computation.3 | async-start | bytes 4718592 | tf_op jit(solution)/shard_map/all_gather | solution.py:108
Sparse Core Ops, SparseCore 0:
  41.4 16.1 all-gather.7
  88.8 37.8 all-gather.5
  128.3 17.3 all-gather.9

commit v6 on v4

--- a/solution.py
+++ b/solution.py
@@ -1,3 +1,4 @@
+import functools
 import math
 
 import jax
@@ -103,24 +104,29 @@
     query_pad = jnp.concatenate(
         [query_rows, jnp.zeros_like(query_rows)], axis=-1
     ).transpose(1, 0, 2)
-    attended = attend(bounds, query_pad, window_rows, fresh_pad)
-    all_heads = lax.all_gather(attended, ("tz", "tc"), axis=1, tiled=True)
     columns = out_weight.shape[1] // (lax.axis_size("tz") * lax.axis_size("tc"))
     my_columns = lax.dynamic_slice_in_dim(out_weight, tensor_rank_index * columns, columns, 1)
-    projected = jnp.dot(all_heads, my_columns, preferred_element_type=jnp.float32)
+    chunk_rows = row_count // ROW_CHUNKS
+    pieces = []
+    for chunk in range(ROW_CHUNKS):
+        attended = attend(bounds, query_pad, window_rows, fresh_pad, chunk * chunk_rows, chunk_rows)
+        all_heads = lax.all_gather(attended, ("tz", "tc"), axis=1, tiled=True)
+        pieces.append(jnp.dot(all_heads, my_columns, preferred_element_type=jnp.float32))
+    projected = jnp.concatenate(pieces, axis=0)
     return projected.astype(jnp.bfloat16)
 
 
 BLOCK_ROWS = 64
-
-
-def attend_kernel(bounds_ref, q_ref, win_ref, fresh_ref, o_ref):
+ROW_CHUNKS = 2
+
+
+def attend_kernel(first_block, bounds_ref, q_ref, win_ref, fresh_ref, o_ref):
     heads, block_rows, _ = q_ref.shape
     stacked = heads * block_rows
     request_count = win_ref.shape[0]
     window = win_ref.shape[1]
     row_count = fresh_ref.shape[0]
-    first_row = pl.program_id(0) * block_rows
+    first_row = (pl.program_id(0) + first_block) * block_rows
     score_scale = HEAD_SIZE ** (-0.5)
     q = q_ref[...].reshape(stacked, 2 * HEAD_SIZE)
     rows = first_row + lax.broadcasted_iota(jnp.int32, (heads, block_rows, 1), 1).reshape(stacked, 1)
@@ -174,18 +180,19 @@
         o_ref[:, h * HEAD_SIZE : (h + 1) * HEAD_SIZE] = result[h * block_rows : (h + 1) * block_rows]
 
 
-def attend(bounds, query_pad, window_rows, fresh_rows):
+def attend(bounds, query_pad, window_rows, fresh_rows, first_row, rows):
     heads, row_count, width = query_pad.shape
-    block_rows = math.gcd(row_count, BLOCK_ROWS)
+    block_rows = math.gcd(rows, BLOCK_ROWS)
+    first_block = first_row // block_rows
     requests, window, _ = window_rows.shape
     return pl.pallas_call(
-        attend_kernel,
-        out_shape=jax.ShapeDtypeStruct((row_count, heads * HEAD_SIZE), jnp.bfloat16),
+        functools.partial(attend_kernel, first_block),
+        out_shape=jax.ShapeDtypeStruct((rows, heads * HEAD_SIZE), jnp.bfloat16),
         grid_spec=pltpu.PrefetchScalarGridSpec(
             num_scalar_prefetch=1,
-            grid=(row_count // block_rows,),
+            grid=(rows // block_rows,),
             in_specs=[
-                pl.BlockSpec((heads, block_rows, width), lambda i, b: (0, i, 0)),
+                pl.BlockSpec((heads, block_rows, width), lambda i, b: (0, i + first_block, 0)),
                 pl.BlockSpec((requests, window, width), lambda i, b: (0, 0, 0)),
                 pl.BlockSpec((row_count, width), lambda i, b: (0, 0)),
             ],

time: 143 us -> 151 us (1.056)
  Pallas kernels: 30.4 us -> 35 us
  local copies, waits for them, and re-layouts: 19 us -> 20.7 us
    pallas_call x1 -> x2, Pallas kernels: 30.4 us -> 35 us  [attend(): pl.pallas_call(functools.partial(attend_kernel, first_block), out_shape=j...]
    unnamed x16 -> x18, local copies, waits for them, and re-layouts: 2.92 us -> 4.65 us
    dot_general x1 -> x2, matrix products: 3.9 us -> 4.54 us  [body(): jnp.dot(all_heads, my_columns, preferred_element_type=jnp.float32)]
    all_gather x1 -> x2, waiting for transfers between devices: 36.2 us -> 36 us  [body(): all_heads = lax.all_gather(attended, ('tz', 'tc'), axis=1, tiled=True)]
  transfers between devices with their start and end apart: 3 -> 4, of which waited for: 3 -> 4; matrix products, arithmetic and copies ran while one was open for 8% -> 9% of each run, Pallas kernels for 0% -> 12%
where the time goes in v6:
time: 151 us; the launch traced here: 150 us
  waiting for transfers between devices  59 us (39%)
  Pallas kernels  35 us (23%)
  local copies, waits for them, and re-layouts  20.7 us (14%)
  between operations  13.3 us (9%)
  matrix products  8.15 us (5%)
  starting transfers between devices  8.01 us (5%)
  other arithmetic  5.85 us (4%)
    all_gather x2, waiting for transfers between devices, body(): all_heads = lax.all_gather(attended, ('tz', 'tc'), axis=1, tiled=True)  36 us
    pallas_call x2, Pallas kernels, attend(): pl.pallas_call(functools.partial(attend_kernel, first_block), out_shape=j...  35 us
    all_to_all x1, waiting for transfers between devices, body(): incoming = lax.all_to_all(outgoing, 'seq', 0, 0, tiled=True)  18.2 us
    all_to_all x1, starting transfers between devices, body(): incoming = lax.all_to_all(outgoing, 'seq', 0, 0, tiled=True)  7.7 us
    gather x1, local copies, waits for them, and re-layouts, body(): both_parts[lax.iota(jnp.int32, both_parts.shape[0])[None, None, :], page_...  5.76 us
    all_gather x1, waiting for transfers between devices, body(): both_parts = lax.all_gather(incoming, 'tc', axis=0)  4.69 us
    unnamed x18, local copies, waits for them, and re-layouts  4.65 us
    dot_general x2, matrix products, body(): jnp.dot(all_heads, my_columns, preferred_element_type=jnp.float32)  4.54 us
  transfers between devices with their start and end apart: 4, of which 4 were waited for; matrix products, arithmetic and copies ran while one was open for 9% of the time, Pallas kernels for 12%

profile of v6, /device:TPU:1, one launch (start us, length us, event | category | flops | bytes accessed | tf_op | source)
XLA Modules:
  0.0 150.0 jit_solution(4254358685991678075)
XLA Ops:
  6.5 0.9 add_select_fusion.1
  7.5 0.7 reshape.106
  8.2 0.1 reshape.110
  8.3 0.9 fusion.8
  9.2 1.2 gather_fusion
  10.5 0.1 reshape.118
  10.7 1.7 %dynamic-slice_bitcast_fusion = bf16[64,64,128]{2,1,0:T(8,128)(2,1)S(1)} fusion(bf16[64,4,128,128]{3,2,1,0:T(8,128)(2,1)} %param.14, s32[]{:T(128)S(6)} %select_n.76, s32[]{:T(128)S(6)} %select_n.78), kind=kLoop, calls=%fused_computation.13 | loop fusion | bytes 2097160 | tf_op jit(solution)/shard_map/dynamic_slice | solution.py:90
  12.3 1.9 %gather_fusion.1 = bf16[80,64,128]{2,1,0:T(8,128)(2,1)} fusion(bf16[64,64,128]{2,1,0:T(8,128)(2,1)S(1)} %dynamic-slice_bitcast_fusion, s32[1024]{0:T(1024)S(1)} %pad_clamp_fusion.1), kind=kCustom, calls=%fused_computation.1 | custom fusion | bytes 2621760 | tf_op jit(solution)/shard_map/gather | solution.py:91
  14.2 7.7 %all-to-all-start = ((bf16[16,5,64,128]{3,2,1,0:T(8,128)(2,1)}), bf16[16,5,64,128]{3,2,1,0:T(8,128)(2,1)S(1)}, u32[]{:S(2)}, u32[]{:S(2)}) async-start(bf16[16,5,64,128]{3,2,1,0:T(8,128)(2,1)} %bitcast.28), calls=%async_computation | async-start | bytes 2621440 | tf_op jit(solution)/shard_map/all_to_all | solution.py:92
  22.0 18.2 %all-to-all-done = bf16[16,5,64,128]{3,2,1,0:T(8,128)(2,1)S(1)} async-done(((bf16[16,5,64,128]{3,2,1,0:T(8,128)(2,1)}), bf16[16,5,64,128]{3,2,1,0:T(8,128)(2,1)S(1)}, u32[]{:S(2)}, u32[]{:S(2)}) %all-to-all-start) | async-done | bytes 1310752 | tf_op jit(solution)/shard_map/all_to_all | solution.py:92
  40.2 1.1 copy-done.3
  41.4 0.6 gather_fusion.2
  42.1 0.1 reshape.132
  42.3 0.2 reduce-window.9
  42.5 2.7 %fusion = f32[768]{0:T(1024)S(1)} fusion(bf16[768,2048]{1,0:T(8,128)(2,1)} %param.9), kind=kLoop, calls=%fused_computation.6 | loop fusion | flops 4717824 | bytes 3148800 | tf_op jit(solution)/shard_map/reduce_sum | solution.py:25
  45.3 2.6 %convolution_convert_fusion = bf16[768,256]{0,1:T(8,128)(2,1)S(1)} fusion(bf16[2048,256]{1,0:T(8,128)(2,1)} %param.11, bf16[768,2048]{1,0:T(8,128)(2,1)S(1)} %copy-done.4, f32[2048]{0:T(1024)S(1)} %copy-done.8, f32[768]{0:T(1024)S(1)} %add_rsqrt_fusion), kind=kOutput, calls=%fused_computation.9 | convolution fusion | flops 811794432 | bytes 4598784 | tf_op jit(solution)/shard_map/dot_general | solution.py:69
  47.9 1.2 copy.12
  49.2 1.4 pad_bitcast_fusion.q_ref
  50.7 1.1 constant_dynamic-slice_fusion
  51.8 1.0 convolution_convert_fusion.3.fresh_ref
  52.9 4.7 %all-gather.9.cloned.1.call-done = bf16[32,5,64,128]{3,2,1,0:T(8,128)(2,1)} async-done(((bf16[16,5,64,128]{3,2,1,0:T(8,128)(2,1)}), bf16[32,5,64,128]{3,2,1,0:T(8,128)(2,1)}) %all-gather.9.cloned.1.call-update) | async-done | bytes 2621456 | tf_op jit(solution)/shard_map/all_gather | solution.py:93
  57.6 5.8 %gather_fusion.3 = bf16[160,64,128]{2,1,0:T(8,128)(2,1)} fusion(bf16[2,16,5,64,128]{4,3,2,1,0:T(8,128)(2,1)} %bitcast.29, s32[160]{0:T(256)S(1)} %reshape.132), kind=kCustom, calls=%fused_computation.3 | custom fusion | bytes 5244800 | tf_op jit(solution)/shard_map/gather | solution.py:95
  63.3 1.7 %copy-done.1 = bf16[160,64,128]{2,1,0:T(8,128)(2,1)S(1)} copy-done((bf16[160,64,128]{2,1,0:T(8,128)(2,1)S(1)}, bf16[160,64,128]{2,1,0:T(8,128)(2,1)}, u32[]{:S(2)}) %copy-start.1) | copy-done | bytes 2621464
  65.1 17.5 %shard_map.91 = bf16[384,256]{1,0:T(8,128)(2,1)} custom-call(s32[10]{0:T(128)S(1)} %pad_add_fusion.bounds_ref, bf16[4,768,128]{2,1,0:T(8,128)(2,1)S(1)} %pad_bitcast_fusion.q_ref, bf16[5,2048,128]{2,1,0:T(8,128)(2,1)S(1)} %bitcast.26, bf16[768,128]{1,0:T(8,128)(2,1)S(1)} %convolution_convert_fusion.3.fresh_ref), custom_call_target="tpu_custom_call" | custom-call | tf_op jit(solution)/shard_map/pallas_call | solution.py:188
  82.6 0.2 all-gather.7.cloned.1.call-start
  82.8 1.7 %copy-done.2 = bf16[160,64,128]{2,1,0:T(8,128)(2,1)S(1)} copy-done((bf16[160,64,128]{2,1,0:T(8,128)(2,1)S(1)}, bf16[160,64,128]{2,1,0:T(8,128)(2,1)}, u32[]{:S(2)}) %copy-start.2) | copy-done | bytes 2621464
  84.6 17.5 %shard_map.92 = bf16[384,256]{1,0:T(8,128)(2,1)} custom-call(s32[10]{0:T(128)S(1)} %pad_add_fusion.bounds_ref, bf16[4,768,128]{2,1,0:T(8,128)(2,1)S(1)} %pad_bitcast_fusion.q_ref, bf16[5,2048,128]{2,1,0:T(8,128)(2,1)S(1)} %bitcast.27, bf16[768,128]{1,0:T(8,128)(2,1)S(1)} %convolution_convert_fusion.3.fresh_ref), custom_call_target="tpu_custom_call" | custom-call | tf_op jit(solution)/shard_map/pallas_call | solution.py:188
  102.1 10.7 %all-gather.5.cloned.1.call-done = bf16[384,2048]{1,0:T(8,128)(2,1)} async-done(((bf16[384,256]{1,0:T(8,128)(2,1)}), bf16[384,2048]{1,0:T(8,128)(2,1)}) %all-gather.5.cloned.1.call-update) | async-done | bytes 1572880 | tf_op jit(solution)/shard_map/all_gather | solution.py:113
  112.8 2.3 %convolution_convert_fusion.2 = bf16[384,256]{1,0:T(8,128)(2,1)S(1)} fusion(bf16[384,2048]{1,0:T(8,128)(2,1)} %all-gather.5.cloned.1.call-done, bf16[2048,2048]{1,0:T(8,128)(2,1)} %param.13, s32[]{:T(128)S(6)} %select_n.86), kind=kOutput, calls=%fused_computation.11 | convolution fusion | flops 402751488 | bytes 2818052 | tf_op jit(solution)/shard_map/dot_general | solution.py:114
  115.1 25.4 %all-gather.7.cloned.1.call-done = bf16[384,2048]{1,0:T(8,128)(2,1)} async-done(((bf16[384,256]{1,0:T(8,128)(2,1)}), bf16[384,2048]{1,0:T(8,128)(2,1)}) %all-gather.7.cloned.1.call-update) | async-done | bytes 1572880 | tf_op jit(solution)/shard_map/all_gather | solution.py:113
  140.4 2.3 %convolution_convert_fusion.1 = bf16[384,256]{1,0:T(8,128)(2,1)S(1)} fusion(bf16[384,2048]{1,0:T(8,128)(2,1)} %all-gather.7.cloned.1.call-done, bf16[2048,2048]{1,0:T(8,128)(2,1)} %param.13, s32[]{:T(128)S(6)} %select_n.86), kind=kOutput, calls=%fused_computation.10 | convolution fusion | flops 402751488 | bytes 2818052 | tf_op jit(solution)/shard_map/dot_general | solution.py:114
  142.7 0.8 pad_maximum_fusion
  (33 shorter events, 0.8 us)
Async XLA Ops:
  6.5 44.1 %copy-start = (bf16[2048,4,128]{2,1,0:T(4,128)(2,1)S(1)}, bf16[2048,4,128]{2,1,0:T(4,128)(2,1)}, u32[]{:S(2)}) copy-start(bf16[2048,4,128]{2,1,0:T(4,128)(2,1)} %param.12) | copy-start | bytes 6291460
  12.3 29.0 %copy-start.6 = (s32[80]{0:T(128)S(1)}, s32[80]{0:T(128)}, u32[]{:S(2)}) copy-start(s32[80]{0:T(128)} %param.17) | copy-start | bytes 964
  12.3 29.9 %copy-start.7 = (s32[80]{0:T(128)S(1)}, s32[80]{0:T(128)}, u32[]{:S(2)}) copy-start(s32[80]{0:T(128)} %param.16) | copy-start | bytes 964
  14.2 31.0 %copy-start.8 = (f32[2048]{0:T(1024)S(1)}, f32[2048]{0:T(1024)}, u32[]{:S(2)}) copy-start(f32[2048]{0:T(1024)} %param.10) | copy-start | bytes 24580
  14.2 26.0 %all-to-all-start = ((bf16[16,5,64,128]{3,2,1,0:T(8,128)(2,1)}), bf16[16,5,64,128]{3,2,1,0:T(8,128)(2,1)S(1)}, u32[]{:S(2)}, u32[]{:S(2)}) async-start(bf16[16,5,64,128]{3,2,1,0:T(8,128)(2,1)} %bitcast.28), calls=%async_computation | async-start | bytes 2621440 | tf_op jit(solution)/shard_map/all_to_all | solution.py:92
  21.9 35.6 %all-gather.9.cloned.1.call-start = ((), (), s32[]{:S(2)}) async-start(), calls=%async_computation.3 | async-start | bytes 3932160 | tf_op jit(solution)/shard_map/all_gather | solution.py:93
  40.2 1.1 copy-start.3
  41.3 71.5 %all-gather.5.cloned.1.call-start = ((), (), s32[]{:S(2)}) async-start(), calls=%async_computation.1 | async-start | bytes 1769472 | tf_op jit(solution)/shard_map/all_gather | solution.py:113
  42.5 2.8 %copy-start.4 = (bf16[768,2048]{1,0:T(8,128)(2,1)S(1)}, bf16[768,2048]{1,0:T(8,128)(2,1)}, u32[]{:S(2)}) copy-start(bf16[768,2048]{1,0:T(8,128)(2,1)} %param.9) | copy-start | bytes 9437188
  49.1 2.8 %copy-start.5 = (bf16[768,2048]{1,0:T(8,128)(2,1)S(1)}, bf16[768,2048]{1,0:T(8,128)(2,1)}, u32[]{:S(2)}) copy-start(bf16[768,2048]{1,0:T(8,128)(2,1)} %param.9) | copy-start | bytes 9437188
  63.3 1.7 %copy-start.1 = (bf16[160,64,128]{2,1,0:T(8,128)(2,1)S(1)}, bf16[160,64,128]{2,1,0:T(8,128)(2,1)}, u32[]{:S(2)}) copy-start(bf16[160,64,128]{2,1,0:T(8,128)(2,1)} %gather_fusion.3) | copy-start | bytes 7864324
  82.6 57.8 %all-gather.7.cloned.1.call-start = ((), (), s32[]{:S(2)}) async-start(), calls=%async_computation.2 | async-start | bytes 1769472 | tf_op jit(solution)/shard_map/all_gather | solution.py:113
  82.8 1.7 %copy-start.2 = (bf16[160,64,128]{2,1,0:T(8,128)(2,1)S(1)}, bf16[160,64,128]{2,1,0:T(8,128)(2,1)}, u32[]{:S(2)}) copy-start(bf16[160,64,128]{2,1,0:T(8,128)(2,1)} %gather_fusion.3) | copy-start | bytes 7864324
Sparse Core Ops, SparseCore 0:
  41.4 16.1 all-gather.8
  82.7 30.0 all-gather.4
  114.5 25.9 all-gather.6

commit v7 on v4

--- a/solution.py
+++ b/solution.py
@@ -25,24 +25,7 @@
     return (widened * factor * norm_gain).astype(jnp.bfloat16)
 
 
-def row_layout(lengths, row_total_count):
-    request_ends = jnp.cumsum(lengths)
-    starts = request_ends - lengths
-    slot_ids = lax.iota(jnp.int32, row_total_count)
-    row_request = jnp.sum((slot_ids[:, None] >= request_ends[None, :]).astype(jnp.int32), axis=1)
-    row_live = slot_ids < request_ends[-1]
-    choose = row_request[:, None] == lax.iota(jnp.int32, lengths.shape[0])[None, :]
-    begins = jnp.sum(jnp.where(choose, starts[None, :], 0), axis=1)
-    return (row_request, row_live, slot_ids - begins)
-
-
-def lookup_rows(table, wanted):
-    table_rows = table.shape[0]
-    matches = wanted[:, None] == lax.iota(jnp.int32, table_rows)[None, :]
-    return jnp.sum(jnp.where(matches[:, :, None], table[None, :, :], 0), axis=1)
-
-
-def body(
+def layer(
     tokens,
     norm_gain,
     query_weight,
@@ -60,10 +43,7 @@
     row_count = tokens.shape[0]
     resident_heads = query_weight.shape[1] // HEAD_SIZE
     key_value_head = tensor_rank_index * resident_heads // (QUERY_HEADS // KEY_VALUE_HEADS)
-    group_count = page_table.shape[0]
-    per_owner = WP // seq_count
     pages_here = cache_pages.shape[0]
-    score_scale = HEAD_SIZE ** (-0.5)
     normed = normalize(tokens, norm_gain)
     query_rows = jnp.dot(normed, query_weight, preferred_element_type=jnp.float32).astype(
         jnp.bfloat16
@@ -204,7 +184,7 @@
         mesh.devices.reshape(seq_size, tensor_size // cores, cores), ("seq", "tz", "tc")
     )
     return jax.shard_map(
-        body,
+        layer,
         mesh=split_mesh,
         in_specs=(
             P("seq", None),

time: 143 us -> 140 us (0.979)
  waiting for transfers between devices: 59.1 us -> 53.3 us
  Pallas kernels: 30.4 us -> 33.8 us
    all_gather x2, waiting for transfers between devices: 40.9 us -> 35.1 us  [the longest x1 30.4 us: layer(): all_heads = lax.all_gather(attended, ('tz', 'tc'), axis=1, tiled=True)]
    pallas_call x1, Pallas kernels: 30.4 us -> 33.8 us  [attend(): pl.pallas_call(attend_kernel, out_shape=jax.ShapeDtypeStruct((row_count,...]
where the time goes in v7:
time: 140 us
  waiting for transfers between devices  53.3 us (38%)
  Pallas kernels  33.8 us (24%)
  local copies, waits for them, and re-layouts  19 us (14%)
  between operations  13.6 us (10%)
  starting transfers between devices  7.78 us (6%)
  matrix products  7.51 us (5%)
  other arithmetic  5.08 us (4%)
    pallas_call x1, Pallas kernels, attend(): pl.pallas_call(attend_kernel, out_shape=jax.ShapeDtypeStruct((row_count,...  33.8 us
    all_gather x1, waiting for transfers between devices, layer(): all_heads = lax.all_gather(attended, ('tz', 'tc'), axis=1, tiled=True)  30.4 us
    all_to_all x1, waiting for transfers between devices, layer(): incoming = lax.all_to_all(outgoing, 'seq', 0, 0, tiled=True)  18.2 us
    all_to_all x1, starting transfers between devices, layer(): incoming = lax.all_to_all(outgoing, 'seq', 0, 0, tiled=True)  7.7 us
    gather x1, local copies, waits for them, and re-layouts, layer(): both_parts[lax.iota(jnp.int32, both_parts.shape[0])[None, None, :], page_...  5.75 us
    all_gather x1, waiting for transfers between devices, layer(): both_parts = lax.all_gather(incoming, 'tc', axis=0)  4.66 us
    dot_general x1, matrix products, layer(): jnp.dot(all_heads, my_columns, preferred_element_type=jnp.float32)  3.9 us
    gather x3, local copies, waits for them, and re-layouts, layer(): outgoing = head_pages[held_slot[all_groups]]  3.17 us
  transfers between devices with their start and end apart: 3, of which 3 were waited for; matrix products, arithmetic and copies ran while one was open for 8% of the time, Pallas kernels for 0%

profile of v7, /device:TPU:1, one launch (start us, length us, event | category | flops | bytes accessed | tf_op | source)
XLA Modules:
  0.0 140.0 jit_solution(15126461426692435975)
XLA Ops:
  6.5 0.9 add_select_fusion.1
  7.5 0.7 reshape.106
  8.2 0.1 reshape.110
  8.3 0.9 fusion.7
  9.2 1.2 gather_fusion
  10.5 0.1 gather.15
  10.5 0.1 reshape.118
  10.7 1.7 %dynamic-slice_bitcast_fusion = bf16[64,64,128]{2,1,0:T(8,128)(2,1)S(1)} fusion(bf16[64,4,128,128]{3,2,1,0:T(8,128)(2,1)} %param.14, s32[]{:T(128)S(6)} %select_n.76, s32[]{:T(128)S(6)} %select_n.78), kind=kLoop, calls=%fused_computation.13 | loop fusion | bytes 2097160 | tf_op jit(solution)/shard_map/dynamic_slice | solution.py:69
  12.3 1.9 %gather_fusion.1 = bf16[80,64,128]{2,1,0:T(8,128)(2,1)} fusion(bf16[64,64,128]{2,1,0:T(8,128)(2,1)S(1)} %dynamic-slice_bitcast_fusion, s32[1024]{0:T(1024)S(1)} %pad_clamp_fusion.1), kind=kCustom, calls=%fused_computation.1 | custom fusion | bytes 2621760 | tf_op jit(solution)/shard_map/gather | solution.py:70
  14.2 7.7 %all-to-all-start = ((bf16[16,5,64,128]{3,2,1,0:T(8,128)(2,1)}), bf16[16,5,64,128]{3,2,1,0:T(8,128)(2,1)S(1)}, u32[]{:S(2)}, u32[]{:S(2)}) async-start(bf16[16,5,64,128]{3,2,1,0:T(8,128)(2,1)} %bitcast.26), calls=%async_computation | async-start | bytes 2621440 | tf_op jit(solution)/shard_map/all_to_all | solution.py:71
  22.0 18.2 %all-to-all-done = bf16[16,5,64,128]{3,2,1,0:T(8,128)(2,1)S(1)} async-done(((bf16[16,5,64,128]{3,2,1,0:T(8,128)(2,1)}), bf16[16,5,64,128]{3,2,1,0:T(8,128)(2,1)S(1)}, u32[]{:S(2)}, u32[]{:S(2)}) %all-to-all-start) | async-done | bytes 1310752 | tf_op jit(solution)/shard_map/all_to_all | solution.py:71
  40.2 1.1 copy-done.2
  41.3 0.1 compare_select_fusion.3
  41.4 0.6 gather_fusion.2
  42.0 0.1 shift-left_or_fusion
  42.1 0.1 reshape.132
  42.2 0.1 dynamic-slice_bitcast_fusion.1
  42.3 0.2 reduce-window.9
  42.5 2.7 %fusion = f32[768]{0:T(1024)S(1)} fusion(bf16[768,2048]{1,0:T(8,128)(2,1)} %param.9), kind=kLoop, calls=%fused_computation.6 | loop fusion | flops 4717824 | bytes 3148800 | tf_op jit(solution)/shard_map/reduce_sum | solution.py:24
  45.2 0.1 copy-done.3
  45.3 2.6 %convolution_convert_fusion.1 = bf16[768,256]{0,1:T(8,128)(2,1)S(1)} fusion(bf16[2048,256]{1,0:T(8,128)(2,1)} %param.11, bf16[768,2048]{1,0:T(8,128)(2,1)S(1)} %copy-done.3, f32[2048]{0:T(1024)S(1)} %copy-done.7, f32[768]{0:T(1024)S(1)} %add_rsqrt_fusion), kind=kOutput, calls=%fused_computation.10 | convolution fusion | flops 811794432 | bytes 4598784 | tf_op jit(solution)/shard_map/dot_general | solution.py:48
  47.9 1.2 copy.12
  49.2 0.1 pad_add_fusion.bounds_ref
  49.2 1.4 %pad_bitcast_fusion.q_ref = bf16[4,768,128]{2,1,0:T(8,128)(2,1)S(1)} fusion(bf16[768,4,64]{2,0,1:T(8,128)(2,1)} %copy.12), kind=kLoop, calls=%fused_computation.14 | loop fusion | bytes 1179648 | tf_op jit(solution)/shard_map/transpose | solution.py:85
  50.7 1.1 constant_dynamic-slice_fusion
  51.8 1.0 convolution_convert_fusion.2.fresh_ref
  52.9 4.7 %all-gather.6.cloned.1.call-done = bf16[32,5,64,128]{3,2,1,0:T(8,128)(2,1)} async-done(((bf16[16,5,64,128]{3,2,1,0:T(8,128)(2,1)}), bf16[32,5,64,128]{3,2,1,0:T(8,128)(2,1)}) %all-gather.6.cloned.1.call-update) | async-done | bytes 2621456 | tf_op jit(solution)/shard_map/all_gather | solution.py:72
  57.6 5.7 %gather_fusion.3 = bf16[160,64,128]{2,1,0:T(8,128)(2,1)} fusion(bf16[2,16,5,64,128]{4,3,2,1,0:T(8,128)(2,1)} %bitcast.27, s32[160]{0:T(256)S(1)} %reshape.132), kind=kCustom, calls=%fused_computation.3 | custom fusion | bytes 5244800 | tf_op jit(solution)/shard_map/gather | solution.py:74
  63.3 1.7 %copy-done.1 = bf16[160,64,128]{2,1,0:T(8,128)(2,1)S(1)} copy-done((bf16[160,64,128]{2,1,0:T(8,128)(2,1)S(1)}, bf16[160,64,128]{2,1,0:T(8,128)(2,1)}, u32[]{:S(2)}) %copy-start.1) | copy-done | bytes 2621464
  65.0 33.8 %shard_map.91 = bf16[768,256]{1,0:T(8,128)(2,1)} custom-call(s32[10]{0:T(128)S(1)} %pad_add_fusion.bounds_ref, bf16[4,768,128]{2,1,0:T(8,128)(2,1)S(1)} %pad_bitcast_fusion.q_ref, bf16[5,2048,128]{2,1,0:T(8,128)(2,1)S(1)} %bitcast.25, bf16[768,128]{1,0:T(8,128)(2,1)S(1)} %convolution_convert_fusion.2.fresh_ref), custom_call_target="tpu_custom_call" | custom-call | tf_op jit(solution)/shard_map/pallas_call | solution.py:161
  98.9 30.4 %all-gather.4.cloned.1.call-done = bf16[768,2048]{1,0:T(8,128)(2,1)} async-done(((bf16[768,256]{1,0:T(8,128)(2,1)}), bf16[768,2048]{1,0:T(8,128)(2,1)}) %all-gather.4.cloned.1.call-update) | async-done | bytes 3145744 | tf_op jit(solution)/shard_map/all_gather | solution.py:87
  129.3 3.9 %convolution_convert_fusion = bf16[768,256]{1,0:T(8,128)(2,1)} fusion(bf16[768,2048]{1,0:T(8,128)(2,1)} %all-gather.4.cloned.1.call-done, bf16[2048,2048]{1,0:T(8,128)(2,1)} %param.13, s32[]{:T(128)S(6)} %select_n.86), kind=kOutput, calls=%fused_computation.9 | convolution fusion | flops 805502976 | bytes 4587524 | tf_op jit(solution)/shard_map/dot_general | solution.py:90
  (25 shorter events, 0.3 us)
Async XLA Ops:
  6.5 44.1 %copy-start = (bf16[2048,4,128]{2,1,0:T(4,128)(2,1)S(1)}, bf16[2048,4,128]{2,1,0:T(4,128)(2,1)}, u32[]{:S(2)}) copy-start(bf16[2048,4,128]{2,1,0:T(4,128)(2,1)} %param.12) | copy-start | bytes 6291460
  12.3 29.0 %copy-start.5 = (s32[80]{0:T(128)S(1)}, s32[80]{0:T(128)}, u32[]{:S(2)}) copy-start(s32[80]{0:T(128)} %param.17) | copy-start | bytes 964
  12.3 29.9 %copy-start.6 = (s32[80]{0:T(128)S(1)}, s32[80]{0:T(128)}, u32[]{:S(2)}) copy-start(s32[80]{0:T(128)} %param.16) | copy-start | bytes 964
  14.2 31.0 %copy-start.7 = (f32[2048]{0:T(1024)S(1)}, f32[2048]{0:T(1024)}, u32[]{:S(2)}) copy-start(f32[2048]{0:T(1024)} %param.10) | copy-start | bytes 24580
  14.2 26.0 %all-to-all-start = ((bf16[16,5,64,128]{3,2,1,0:T(8,128)(2,1)}), bf16[16,5,64,128]{3,2,1,0:T(8,128)(2,1)S(1)}, u32[]{:S(2)}, u32[]{:S(2)}) async-start(bf16[16,5,64,128]{3,2,1,0:T(8,128)(2,1)} %bitcast.26), calls=%async_computation | async-start | bytes 2621440 | tf_op jit(solution)/shard_map/all_to_all | solution.py:71
  21.9 35.6 %all-gather.6.cloned.1.call-start = ((), (), s32[]{:S(2)}) async-start(), calls=%async_computation.2 | async-start | bytes 3932160 | tf_op jit(solution)/shard_map/all_gather | solution.py:72
  40.2 1.1 copy-start.2
  41.3 88.0 %all-gather.4.cloned.1.call-start = ((), (), s32[]{:S(2)}) async-start(), calls=%async_computation.1 | async-start | bytes 3538944 | tf_op jit(solution)/shard_map/all_gather | solution.py:87
  42.5 2.8 %copy-start.3 = (bf16[768,2048]{1,0:T(8,128)(2,1)S(1)}, bf16[768,2048]{1,0:T(8,128)(2,1)}, u32[]{:S(2)}) copy-start(bf16[768,2048]{1,0:T(8,128)(2,1)} %param.9) | copy-start | bytes 9437188
  49.1 2.8 %copy-start.4 = (bf16[768,2048]{1,0:T(8,128)(2,1)S(1)}, bf16[768,2048]{1,0:T(8,128)(2,1)}, u32[]{:S(2)}) copy-start(bf16[768,2048]{1,0:T(8,128)(2,1)} %param.9) | copy-start | bytes 9437188
  63.3 1.7 %copy-start.1 = (bf16[160,64,128]{2,1,0:T(8,128)(2,1)S(1)}, bf16[160,64,128]{2,1,0:T(8,128)(2,1)}, u32[]{:S(2)}) copy-start(bf16[160,64,128]{2,1,0:T(8,128)(2,1)} %gather_fusion.3) | copy-start | bytes 7864324
Sparse Core Ops, SparseCore 0:
  41.4 16.1 all-gather.5
  99.0 30.2 all-gather.3

commit v8 on v7

--- a/solution.py
+++ b/solution.py
@@ -69,10 +69,12 @@
     head_pages = lax.dynamic_slice_in_dim(head_pages, core_index * page_part, page_part, 1)
     outgoing = head_pages[held_slot[all_groups]]
     incoming = lax.all_to_all(outgoing, "seq", 0, 0, tiled=True)
-    both_parts = lax.all_gather(incoming, "tc", axis=0)
+    core_count = lax.axis_size("tc")
+    partner = lax.ppermute(incoming, "tc", [(0, 1), (1, 0)])
+    both_parts = jnp.stack([incoming, partner])
     page_source = holder[my_groups]
     window_rows = both_parts[
-        lax.iota(jnp.int32, both_parts.shape[0])[None, None, :],
+        ((lax.iota(jnp.int32, core_count) + core_index) % core_count)[None, None, :],
         page_source[:, :, None],
         lax.iota(jnp.int32, DEVICE_REQUESTS)[:, None, None],
     ]
@@ -91,7 +93,7 @@
     return projected.astype(jnp.bfloat16)
 
 
-BLOCK_ROWS = 64
+BLOCK_ROWS = 32
 
 
 def attend_kernel(bounds_ref, q_ref, win_ref, fresh_ref, o_ref):

time: 140 us -> 139 us (level)
  waiting for transfers between devices: 53.3 us -> 43.2 us
  starting transfers between devices: 7.78 us -> 11.3 us
  other arithmetic: 5.08 us -> 8.32 us
  Pallas kernels: 33.8 us -> 35.6 us
    all_gather x1 -> x0, waiting for transfers between devices: 4.66 us -> none  [layer(): both_parts = lax.all_gather(incoming, 'tc', axis=0)]
    all_to_all x1, waiting for transfers between devices: 18.2 us -> 14.5 us  [layer(): incoming = lax.all_to_all(outgoing, 'seq', 0, 0, tiled=True)]
    ppermute x0 -> x1, starting transfers between devices: none -> 3.49 us  [layer(): partner = lax.ppermute(incoming, 'tc', [(0, 1), (1, 0)])]
    another operation x1 -> x2, other arithmetic: 0.18 us -> 3.64 us  [the longest x1 3.46 us: layer(): both_parts = jnp.stack([incoming, partner])]
    pallas_call x1, Pallas kernels: 33.8 us -> 35.6 us  [attend(): pl.pallas_call(attend_kernel, out_shape=jax.ShapeDtypeStruct((row_count,...]
    all_gather x1, waiting for transfers between devices: 30.4 us -> 28.7 us  [layer(): all_heads = lax.all_gather(attended, ('tz', 'tc'), axis=1, tiled=True)]
    unnamed x16 -> x12, local copies, waits for them, and re-layouts: 2.92 us -> 1.76 us
  transfers between devices with their start and end apart: 3 -> 3, of which waited for: 3 -> 2; matrix products, arithmetic and copies ran while one was open for 8% -> 9% of each run, Pallas kernels for 0% -> 0%
where the time goes in v8:
time: 139 us; the launch traced here: 138 us
  waiting for transfers between devices  43.2 us (31%)
  Pallas kernels  35.6 us (26%)
  local copies, waits for them, and re-layouts  17.8 us (13%)
  between operations  13.6 us (10%)
  starting transfers between devices  11.3 us (8%)
  matrix products  8.38 us (6%)
  other arithmetic  8.32 us (6%)
    pallas_call x1, Pallas kernels, attend(): pl.pallas_call(attend_kernel, out_shape=jax.ShapeDtypeStruct((row_count,...  35.6 us
    all_gather x1, waiting for transfers between devices, layer(): all_heads = lax.all_gather(attended, ('tz', 'tc'), axis=1, tiled=True)  28.7 us
    all_to_all x1, waiting for transfers between devices, layer(): incoming = lax.all_to_all(outgoing, 'seq', 0, 0, tiled=True)  14.5 us
    all_to_all x1, starting transfers between devices, layer(): incoming = lax.all_to_all(outgoing, 'seq', 0, 0, tiled=True)  7.75 us
    gather x1, local copies, waits for them, and re-layouts, layer(): both_parts[((lax.iota(jnp.int32, core_count) + core_index) % core_count)[...  5.74 us
    dot_general x1, matrix products, layer(): jnp.dot(all_heads, my_columns, preferred_element_type=jnp.float32)  3.9 us
    ppermute x1, starting transfers between devices, layer(): partner = lax.ppermute(incoming, 'tc', [(0, 1), (1, 0)])  3.49 us
    another operation x1, other arithmetic, layer(): both_parts = jnp.stack([incoming, partner])  3.46 us
  transfers between devices with their start and end apart: 3, of which 2 were waited for; matrix products, arithmetic and copies ran while one was open for 9% of the time, Pallas kernels for 0%

profile of v8, /device:TPU:1, one launch (start us, length us, event | category | flops | bytes accessed | tf_op | source)
XLA Modules:
  0.0 138.1 jit_solution(2929656030088869436)
XLA Ops:
  6.5 0.9 add_select_fusion.1
  7.5 0.7 reshape.111
  8.2 0.1 reshape.115
  8.3 0.9 fusion.7
  9.2 1.2 gather_fusion
  10.5 0.1 gather.15
  10.5 0.1 reshape.123
  10.7 1.7 %dynamic-slice_bitcast_fusion = bf16[64,64,128]{2,1,0:T(8,128)(2,1)S(1)} fusion(bf16[64,4,128,128]{3,2,1,0:T(8,128)(2,1)} %param.14, s32[]{:T(128)S(6)} %select_n.91, s32[]{:T(128)S(6)} %select_n.93), kind=kLoop, calls=%fused_computation.14 | loop fusion | bytes 2097160 | tf_op jit(solution)/shard_map/dynamic_slice | solution.py:69
  12.3 1.9 %gather_fusion.1 = bf16[80,64,128]{2,1,0:T(8,128)(2,1)} fusion(bf16[64,64,128]{2,1,0:T(8,128)(2,1)S(1)} %dynamic-slice_bitcast_fusion, s32[1024]{0:T(1024)S(1)} %pad_clamp_fusion.1), kind=kCustom, calls=%fused_computation.1 | custom fusion | bytes 2621760 | tf_op jit(solution)/shard_map/gather | solution.py:70
  14.2 7.7 %all-to-all-start = ((bf16[16,5,64,128]{3,2,1,0:T(8,128)(2,1)}), bf16[16,5,64,128]{3,2,1,0:T(8,128)(2,1)}, u32[]{:S(2)}, u32[]{:S(2)}) async-start(bf16[16,5,64,128]{3,2,1,0:T(8,128)(2,1)} %bitcast.27), calls=%async_computation | async-start | bytes 2621440 | tf_op jit(solution)/shard_map/all_to_all | solution.py:71
  22.0 0.0 all-gather.2.cloned.1.call-start
  22.0 0.1 dynamic-slice_bitcast_fusion.1
  22.1 0.2 reduce-window.9
  22.3 0.1 compare_select_fusion.3
  22.4 0.6 gather_fusion.2
  23.0 0.1 shift-left_or_fusion
  23.0 0.1 reshape.137
  23.2 2.6 %fusion = f32[768]{0:T(1024)S(1)} fusion(bf16[768,2048]{1,0:T(8,128)(2,1)} %param.9), kind=kLoop, calls=%fused_computation.6 | loop fusion | flops 4717824 | bytes 3148800 | tf_op jit(solution)/shard_map/reduce_sum | solution.py:24
  25.8 14.5 %all-to-all-done = bf16[16,5,64,128]{3,2,1,0:T(8,128)(2,1)} async-done(((bf16[16,5,64,128]{3,2,1,0:T(8,128)(2,1)}), bf16[16,5,64,128]{3,2,1,0:T(8,128)(2,1)}, u32[]{:S(2)}, u32[]{:S(2)}) %all-to-all-start) | async-done | bytes 1310752 | tf_op jit(solution)/shard_map/all_to_all | solution.py:71
  40.3 3.5 %collective-permute-start = (bf16[16,5,64,128]{3,2,1,0:T(8,128)(2,1)}, bf16[16,5,64,128]{3,2,1,0:T(8,128)(2,1)}, u32[]{:S(2)}, u32[]{:S(2)}) collective-permute-start(bf16[16,5,64,128]{3,2,1,0:T(8,128)(2,1)} %all-to-all-done), channel_id=1, source_target_pairs={{0,1},{1,0},{2,3},{3,2},{4,5},{5,4},{6,7},{7,6},{8,9},{9,8},{10,11... | collective-permute-start | bytes 3932168 | tf_op jit(solution)/shard_map/ppermute | solution.py:73
  43.8 3.4 %convolution_convert_fusion.1 = bf16[768,256]{0,1:T(8,128)(2,1)S(1)} fusion(bf16[2048,256]{1,0:T(8,128)(2,1)} %param.11, bf16[768,2048]{1,0:T(8,128)(2,1)} %param.9, f32[2048]{0:T(1024)S(1)} %copy-done.5, f32[768]{0:T(1024)S(1)} %add_rsqrt_fusion), kind=kOutput, calls=%fused_computation.11 | convolution fusion | flops 811794432 | bytes 4598784 | tf_op jit(solution)/shard_map/dot_general | solution.py:48
  47.2 1.2 copy.10
  48.4 0.1 pad_add_fusion.bounds_ref
  48.5 1.4 %pad_bitcast_fusion.q_ref = bf16[4,768,128]{2,1,0:T(8,128)(2,1)S(1)} fusion(bf16[768,4,64]{2,0,1:T(8,128)(2,1)} %copy.10), kind=kLoop, calls=%fused_computation.15 | loop fusion | bytes 1179648 | tf_op jit(solution)/shard_map/transpose | solution.py:87
  49.9 1.1 constant_dynamic-slice_fusion
  51.1 1.0 convolution_convert_fusion.2.fresh_ref
  52.1 3.5 %pad_maximum_fusion = bf16[2,16,5,64,128]{4,3,2,1,0:T(8,128)(2,1)} fusion(bf16[1,16,5,64,128]{4,3,2,1,0:T(8,128)(2,1)} %bitcast.7, bf16[1,16,5,64,128]{4,3,2,1,0:T(8,128)(2,1)} %bitcast.6), kind=kLoop, calls=%fused_computation.9 | loop fusion | flops 1310720 | bytes 5242880 | tf_op jit(solution)/shard_map/stack | solution.py:74
  55.6 5.7 %gather_fusion.3 = bf16[160,64,128]{2,1,0:T(8,128)(2,1)} fusion(bf16[2,16,5,64,128]{4,3,2,1,0:T(8,128)(2,1)} %pad_maximum_fusion, s32[160]{0:T(256)S(1)} %reshape.137), kind=kCustom, calls=%fused_computation.3 | custom fusion | bytes 5244800 | tf_op jit(solution)/shard_map/gather | solution.py:76
  61.4 1.7 %copy-done.1 = bf16[160,64,128]{2,1,0:T(8,128)(2,1)S(1)} copy-done((bf16[160,64,128]{2,1,0:T(8,128)(2,1)S(1)}, bf16[160,64,128]{2,1,0:T(8,128)(2,1)}, u32[]{:S(2)}) %copy-start.1) | copy-done | bytes 2621464
  63.1 35.6 %shard_map.91 = bf16[768,256]{1,0:T(8,128)(2,1)} custom-call(s32[10]{0:T(128)S(1)} %pad_add_fusion.bounds_ref, bf16[4,768,128]{2,1,0:T(8,128)(2,1)S(1)} %pad_bitcast_fusion.q_ref, bf16[5,2048,128]{2,1,0:T(8,128)(2,1)S(1)} %bitcast.26, bf16[768,128]{1,0:T(8,128)(2,1)S(1)} %convolution_convert_fusion.2.fresh_ref), custom_call_target="tpu_custom_call" | custom-call | tf_op jit(solution)/shard_map/pallas_call | solution.py:163
  98.7 28.7 %all-gather.2.cloned.1.call-done = bf16[768,2048]{1,0:T(8,128)(2,1)} async-done(((bf16[768,256]{1,0:T(8,128)(2,1)}), bf16[768,2048]{1,0:T(8,128)(2,1)}) %all-gather.2.cloned.1.call-update) | async-done | bytes 3145744 | tf_op jit(solution)/shard_map/all_gather | solution.py:89
  127.4 3.9 %convolution_convert_fusion = bf16[768,256]{1,0:T(8,128)(2,1)} fusion(bf16[768,2048]{1,0:T(8,128)(2,1)} %all-gather.2.cloned.1.call-done, bf16[2048,2048]{1,0:T(8,128)(2,1)} %param.13, s32[]{:T(128)S(6)} %select_n.103), kind=kOutput, calls=%fused_computation.10 | convolution fusion | flops 805502976 | bytes 4587524 | tf_op jit(solution)/shard_map/dot_general | solution.py:92
  (21 shorter events, 0.1 us)
Async XLA Ops:
  6.5 43.4 %copy-start = (bf16[2048,4,128]{2,1,0:T(4,128)(2,1)S(1)}, bf16[2048,4,128]{2,1,0:T(4,128)(2,1)}, u32[]{:S(2)}) copy-start(bf16[2048,4,128]{2,1,0:T(4,128)(2,1)} %param.12) | copy-start | bytes 6291460
  12.3 9.7 %copy-start.4 = (s32[80]{0:T(128)S(1)}, s32[80]{0:T(128)}, u32[]{:S(2)}) copy-start(s32[80]{0:T(128)} %param.16) | copy-start | bytes 964
  12.3 10.0 %copy-start.3 = (s32[80]{0:T(128)S(1)}, s32[80]{0:T(128)}, u32[]{:S(2)}) copy-start(s32[80]{0:T(128)} %param.17) | copy-start | bytes 964
  14.2 29.6 %copy-start.5 = (f32[2048]{0:T(1024)S(1)}, f32[2048]{0:T(1024)}, u32[]{:S(2)}) copy-start(f32[2048]{0:T(1024)} %param.10) | copy-start | bytes 24580
  14.2 26.1 %all-to-all-start = ((bf16[16,5,64,128]{3,2,1,0:T(8,128)(2,1)}), bf16[16,5,64,128]{3,2,1,0:T(8,128)(2,1)}, u32[]{:S(2)}, u32[]{:S(2)}) async-start(bf16[16,5,64,128]{3,2,1,0:T(8,128)(2,1)} %bitcast.27), calls=%async_computation | async-start | bytes 2621440 | tf_op jit(solution)/shard_map/all_to_all | solution.py:71
  22.0 105.4 %all-gather.2.cloned.1.call-start = ((), (), s32[]{:S(2)}) async-start(), calls=%async_computation.1 | async-start | bytes 3538944 | tf_op jit(solution)/shard_map/all_gather | solution.py:89
  40.3 11.8 %collective-permute-start = (bf16[16,5,64,128]{3,2,1,0:T(8,128)(2,1)}, bf16[16,5,64,128]{3,2,1,0:T(8,128)(2,1)}, u32[]{:S(2)}, u32[]{:S(2)}) collective-permute-start(bf16[16,5,64,128]{3,2,1,0:T(8,128)(2,1)} %all-to-all-done), channel_id=1, source_target_pairs={{0,1},{1,0},{2,3},{3,2},{4,5},{5,4},{6,7},{7,6},{8,9},{9,8},{10,11... | collective-permute-start | bytes 3932168 | tf_op jit(solution)/shard_map/ppermute | solution.py:73
  48.4 2.7 %copy-start.2 = (bf16[768,2048]{1,0:T(8,128)(2,1)S(1)}, bf16[768,2048]{1,0:T(8,128)(2,1)}, u32[]{:S(2)}) copy-start(bf16[768,2048]{1,0:T(8,128)(2,1)} %param.9) | copy-start | bytes 9437188
  61.4 1.7 %copy-start.1 = (bf16[160,64,128]{2,1,0:T(8,128)(2,1)S(1)}, bf16[160,64,128]{2,1,0:T(8,128)(2,1)}, u32[]{:S(2)}) copy-start(bf16[160,64,128]{2,1,0:T(8,128)(2,1)} %gather_fusion.3) | copy-start | bytes 7864324
Sparse Core Ops, SparseCore 0:
  98.8 28.5 all-gather.1

commit v9 on v8

--- a/solution.py
+++ b/solution.py
@@ -86,14 +86,37 @@
         [query_rows, jnp.zeros_like(query_rows)], axis=-1
     ).transpose(1, 0, 2)
     attended = attend(bounds, query_pad, window_rows, fresh_pad)
-    all_heads = lax.all_gather(attended, ("tz", "tc"), axis=1, tiled=True)
-    columns = out_weight.shape[1] // (lax.axis_size("tz") * lax.axis_size("tc"))
-    my_columns = lax.dynamic_slice_in_dim(out_weight, tensor_rank_index * columns, columns, 1)
-    projected = jnp.dot(all_heads, my_columns, preferred_element_type=jnp.float32)
-    return projected.astype(jnp.bfloat16)
-
-
-BLOCK_ROWS = 32
+    swap = [(0, 1), (1, 0)]
+    z_count = lax.axis_size("tz")
+    z_index = lax.axis_index("tz")
+    partner_heads = lax.ppermute(attended, "tc", swap)
+    first_core = core_index == 0
+    chip_heads = jnp.where(
+        first_core,
+        jnp.concatenate([attended, partner_heads], axis=1),
+        jnp.concatenate([partner_heads, attended], axis=1),
+    )
+    half_rows = row_count // core_count
+    my_half = lax.dynamic_slice_in_dim(chip_heads, core_index * half_rows, half_rows, 0)
+    sent = jnp.broadcast_to(my_half[None], (z_count,) + my_half.shape)
+    chips_heads = lax.all_to_all(sent, "tz", 0, 0, tiled=True)
+    chip_width = out_weight.shape[1] // z_count
+    chip_columns = lax.dynamic_slice_in_dim(out_weight, z_index * chip_width, chip_width, 1)
+    chip_columns = chip_columns.reshape(z_count, my_half.shape[1], chip_width)
+    half_out = jnp.einsum(
+        "zrj,zjn->rn", chips_heads, chip_columns, preferred_element_type=jnp.float32
+    ).astype(jnp.bfloat16)
+    columns = chip_width // core_count
+    keep = lax.dynamic_slice_in_dim(half_out, core_index * columns, columns, 1)
+    give = lax.dynamic_slice_in_dim(half_out, (1 - core_index) * columns, columns, 1)
+    got = lax.ppermute(give, "tc", swap)
+    projected = jnp.where(
+        first_core, jnp.concatenate([keep, got], axis=0), jnp.concatenate([got, keep], axis=0)
+    )
+    return projected
+
+
+BLOCK_ROWS = 64
 
 
 def attend_kernel(bounds_ref, q_ref, win_ref, fresh_ref, o_ref):

time: 139 us -> 125 us (0.90)
  between operations: 13.6 us -> 0.21 us
  waiting for transfers between devices: 43.2 us -> 34.8 us
  starting transfers between devices: 11.3 us -> 17.8 us
  local copies, waits for them, and re-layouts: 17.8 us -> 22.2 us
  Pallas kernels: 35.6 us -> 33.1 us
    all_gather x1 -> x0, waiting for transfers between devices: 28.7 us -> none  [layer(): all_heads = lax.all_gather(attended, ('tz', 'tc'), axis=1, tiled=True)]
    all_to_all x0 -> x1, waiting for transfers between devices: none -> 17.4 us  [layer(): chips_heads = lax.all_to_all(sent, 'tz', 0, 0, tiled=True)]
    all_to_all x0 -> x1, starting transfers between devices: none -> 5.02 us  [layer(): chips_heads = lax.all_to_all(sent, 'tz', 0, 0, tiled=True)]
    dynamic_slice x0 -> x2, local copies, waits for them, and re-layouts: none -> 3.11 us  [the longest x1 3.07 us: layer(): lax.dynamic_slice_in_dim(out_weight, z_index * chip_width, chip_width, 1)]
    ppermute x0 -> x2, waiting for transfers between devices: none -> 2.77 us  [the longest x1 1.7 us: layer(): partner_heads = lax.ppermute(attended, 'tc', swap)]
    pallas_call x1, Pallas kernels: 35.6 us -> 33.1 us  [attend(): pl.pallas_call(attend_kernel, out_shape=jax.ShapeDtypeStruct((row_count,...]
    ppermute x0 -> x2, starting transfers between devices: none -> 1.5 us  [the longest x1 1.41 us: layer(): got = lax.ppermute(give, 'tc', swap)]
  transfers between devices with their start and end apart: 3 -> 5, of which waited for: 2 -> 4; matrix products, arithmetic and copies ran while one was open for 9% -> 12% of each run, Pallas kernels for 0% -> 0%
where the time goes in v9:
time: 125 us
  waiting for transfers between devices  34.8 us (28%)
  Pallas kernels  33.1 us (26%)
  local copies, waits for them, and re-layouts  22.2 us (18%)
  starting transfers between devices  17.8 us (14%)
  other arithmetic  9.33 us (7%)
  matrix products  7.52 us (6%)
    pallas_call x1, Pallas kernels, attend(): pl.pallas_call(attend_kernel, out_shape=jax.ShapeDtypeStruct((row_count,...  33.1 us
    all_to_all x1, waiting for transfers between devices, layer(): chips_heads = lax.all_to_all(sent, 'tz', 0, 0, tiled=True)  17.4 us
    all_to_all x1, waiting for transfers between devices, layer(): incoming = lax.all_to_all(outgoing, 'seq', 0, 0, tiled=True)  14.6 us
    all_to_all x1, starting transfers between devices, layer(): incoming = lax.all_to_all(outgoing, 'seq', 0, 0, tiled=True)  7.75 us
    gather x1, local copies, waits for them, and re-layouts, layer(): both_parts[((lax.iota(jnp.int32, core_count) + core_index) % core_count)[...  5.75 us
    all_to_all x1, starting transfers between devices, layer(): chips_heads = lax.all_to_all(sent, 'tz', 0, 0, tiled=True)  5.02 us
    ppermute x1, starting transfers between devices, layer(): partner = lax.ppermute(incoming, 'tc', [(0, 1), (1, 0)])  3.49 us
    another operation x1, other arithmetic, layer(): both_parts = jnp.stack([incoming, partner])  3.47 us
  transfers between devices with their start and end apart: 5, of which 4 were waited for; matrix products, arithmetic and copies ran while one was open for 12% of the time, Pallas kernels for 0%

profile of v9, /device:TPU:1, one launch (start us, length us, event | category | flops | bytes accessed | tf_op | source)
XLA Modules:
  0.0 124.9 jit_solution(721550792048565242)
XLA Ops:
  0.0 0.9 add_select_fusion.1
  0.9 0.7 reshape.115
  1.8 0.9 fusion.10
  2.7 1.2 gather_fusion
  4.1 1.7 %dynamic-slice_bitcast_fusion = bf16[64,64,128]{2,1,0:T(8,128)(2,1)S(1)} fusion(bf16[64,4,128,128]{3,2,1,0:T(8,128)(2,1)} %param.14, s32[]{:T(128)S(6)} %select_n.118, s32[]{:T(128)S(6)} %select_n.120), kind=kLoop, calls=%fused_computation.14 | loop fusion | bytes 2097160 | tf_op jit(solution)/shard_map/dynamic_slice | solution.py:69
  5.8 1.9 %gather_fusion.1 = bf16[80,64,128]{2,1,0:T(8,128)(2,1)} fusion(bf16[64,64,128]{2,1,0:T(8,128)(2,1)S(1)} %dynamic-slice_bitcast_fusion, s32[1024]{0:T(1024)S(1)} %pad_clamp_fusion.1), kind=kCustom, calls=%fused_computation.1 | custom fusion | bytes 2621760 | tf_op jit(solution)/shard_map/gather | solution.py:70
  7.7 7.7 %all-to-all-start = ((bf16[16,5,64,128]{3,2,1,0:T(8,128)(2,1)}), bf16[16,5,64,128]{3,2,1,0:T(8,128)(2,1)}, u32[]{:S(2)}, u32[]{:S(2)}) async-start(bf16[16,5,64,128]{3,2,1,0:T(8,128)(2,1)} %bitcast.33), calls=%async_computation | async-start | bytes 2621440 | tf_op jit(solution)/shard_map/all_to_all | solution.py:71
  15.5 0.2 reduce-window.9
  15.8 0.6 gather_fusion.2
  16.5 0.1 reshape.142
  16.6 2.6 %fusion = f32[768]{0:T(1024)S(1)} fusion(bf16[768,2048]{1,0:T(8,128)(2,1)} %param.9), kind=kLoop, calls=%fused_computation.6 | loop fusion | flops 4717824 | bytes 3148800 | tf_op jit(solution)/shard_map/reduce_sum | solution.py:24
  19.2 14.6 %all-to-all-done = bf16[16,5,64,128]{3,2,1,0:T(8,128)(2,1)} async-done(((bf16[16,5,64,128]{3,2,1,0:T(8,128)(2,1)}), bf16[16,5,64,128]{3,2,1,0:T(8,128)(2,1)}, u32[]{:S(2)}, u32[]{:S(2)}) %all-to-all-start) | async-done | bytes 1310752 | tf_op jit(solution)/shard_map/all_to_all | solution.py:71
  33.8 3.5 %collective-permute-start = (bf16[16,5,64,128]{3,2,1,0:T(8,128)(2,1)}, bf16[16,5,64,128]{3,2,1,0:T(8,128)(2,1)}, u32[]{:S(2)}, u32[]{:S(2)}) collective-permute-start(bf16[16,5,64,128]{3,2,1,0:T(8,128)(2,1)} %all-to-all-done), channel_id=1, source_target_pairs={{0,1},{1,0},{2,3},{3,2},{4,5},{5,4},{6,7},{7,6},{8,9},{9,8},{10,11... | collective-permute-start | bytes 3932168 | tf_op jit(solution)/shard_map/ppermute | solution.py:73
  37.3 3.4 %convolution_convert_fusion = bf16[768,256]{0,1:T(8,128)(2,1)S(1)} fusion(bf16[2048,256]{1,0:T(8,128)(2,1)} %param.11, bf16[768,2048]{1,0:T(8,128)(2,1)} %param.9, f32[2048]{0:T(1024)S(1)} %copy-done.5, f32[768]{0:T(1024)S(1)} %add_rsqrt_fusion), kind=kOutput, calls=%fused_computation.12 | convolution fusion | flops 811794432 | bytes 4598784 | tf_op jit(solution)/shard_map/dot_general | solution.py:48
  40.7 1.2 copy.10
  41.9 1.4 %pad_bitcast_fusion.q_ref = bf16[4,768,128]{2,1,0:T(8,128)(2,1)S(1)} fusion(bf16[768,4,64]{2,0,1:T(8,128)(2,1)} %copy.10), kind=kLoop, calls=%fused_computation.19 | loop fusion | bytes 1179648 | tf_op jit(solution)/shard_map/transpose | solution.py:87
  43.4 1.1 constant_dynamic-slice_fusion.3
  44.5 1.0 convolution_convert_fusion.1.fresh_ref
  45.6 3.5 %pad_maximum_fusion = bf16[2,16,5,64,128]{4,3,2,1,0:T(8,128)(2,1)} fusion(bf16[1,16,5,64,128]{4,3,2,1,0:T(8,128)(2,1)} %bitcast.7, bf16[1,16,5,64,128]{4,3,2,1,0:T(8,128)(2,1)} %bitcast.6), kind=kLoop, calls=%fused_computation.9 | loop fusion | flops 1310720 | bytes 5242880 | tf_op jit(solution)/shard_map/stack | solution.py:74
  49.1 5.8 %gather_fusion.3 = bf16[160,64,128]{2,1,0:T(8,128)(2,1)} fusion(bf16[2,16,5,64,128]{4,3,2,1,0:T(8,128)(2,1)} %pad_maximum_fusion, s32[160]{0:T(256)S(1)} %reshape.142), kind=kCustom, calls=%fused_computation.3 | custom fusion | bytes 5244800 | tf_op jit(solution)/shard_map/gather | solution.py:76
  54.8 1.7 %copy-done.1 = bf16[160,64,128]{2,1,0:T(8,128)(2,1)S(1)} copy-done((bf16[160,64,128]{2,1,0:T(8,128)(2,1)S(1)}, bf16[160,64,128]{2,1,0:T(8,128)(2,1)}, u32[]{:S(2)}) %copy-start.1) | copy-done | bytes 2621464
  56.6 33.1 %shard_map.91 = bf16[768,256]{1,0:T(8,128)(2,1)S(1)} custom-call(s32[10]{0:T(128)S(1)} %pad_add_fusion.bounds_ref, bf16[4,768,128]{2,1,0:T(8,128)(2,1)S(1)} %pad_bitcast_fusion.q_ref, bf16[5,2048,128]{2,1,0:T(8,128)(2,1)S(1)} %bitcast.32, bf16[768,128]{1,0:T(8,128)(2,1)S(1)} %convolution_convert_fusion.1.fresh_ref), custom_call_target="tpu_custom_call" | custom-call | tf_op jit(solution)/shard_map/pallas_call | solution.py:186
  89.8 1.7 %collective-permute-done.1 = bf16[768,256]{1,0:T(8,128)(2,1)S(1)} collective-permute-done((bf16[768,256]{1,0:T(8,128)(2,1)S(1)}, bf16[768,256]{1,0:T(8,128)(2,1)S(1)}, u32[]{:S(2)}, u32[]{:S(2)}) %collective-permute-start.1) | collective-permute-done | bytes 393248 | tf_op jit(solution)/shard_map/ppermute | solution.py:92
  91.5 0.1 fusion.7
  91.6 1.3 %broadcast_in_dim.16 = bf16[4,384,512]{2,1,0:T(8,128)(2,1)} broadcast(bf16[384,512]{1,0:T(8,128)(2,1)S(1)} %fusion.7), dimensions={1,2} | broadcast | bytes 1966080 | tf_op jit(solution)/shard_map/broadcast_in_dim | solution.py:101
  92.9 5.0 %all-to-all-start.1 = ((bf16[4,384,512]{2,1,0:T(8,128)(2,1)}), bf16[4,384,512]{2,1,0:T(8,128)(2,1)}, u32[]{:S(2)}, u32[]{:S(2)}) async-start(bf16[4,384,512]{2,1,0:T(8,128)(2,1)} %broadcast_in_dim.16), calls=%async_computation.1 | async-start | bytes 3145728 | tf_op jit(solution)/shard_map/all_to_all | solution.py:102
  97.9 3.1 %constant_dynamic-slice_fusion.2 = bf16[2048,512]{1,0:T(8,128)(2,1)} fusion(bf16[2048,2048]{1,0:T(8,128)(2,1)} %param.13, s32[]{:T(128)S(6)} %select_n.132), kind=kLoop, calls=%fused_computation.50 | loop fusion | bytes 4194308 | tf_op jit(solution)/shard_map/dynamic_slice | solution.py:104
  101.0 17.4 %all-to-all-done.1 = bf16[4,384,512]{2,1,0:T(8,128)(2,1)} async-done(((bf16[4,384,512]{2,1,0:T(8,128)(2,1)}), bf16[4,384,512]{2,1,0:T(8,128)(2,1)}, u32[]{:S(2)}, u32[]{:S(2)}) %all-to-all-start.1) | async-done | bytes 1572896 | tf_op jit(solution)/shard_map/all_to_all | solution.py:102
  118.4 3.0 %fusion.3 = bf16[384,512]{1,0:T(8,128)(2,1)S(1)} fusion(bf16[4,384,512]{2,1,0:T(8,128)(2,1)} %all-to-all-done.1, bf16[4,512,512]{2,1,0:T(8,128)(2,1)} %bitcast.34), kind=kOutput, calls=%fused_computation.11 | convolution fusion | flops 805502976 | bytes 4063232 | tf_op jit(solution)/shard_map/zrj,zjn->rn/dot_general | solution.py:106
  121.5 1.4 %collective-permute-start.2 = (bf16[384,256]{1,0:T(8,128)(2,1)S(1)}, bf16[384,256]{1,0:T(8,128)(2,1)S(1)}, u32[]{:S(2)}, u32[]{:S(2)}) collective-permute-start(bf16[384,256]{1,0:T(8,128)(2,1)S(1)} %get-tuple-element.8), channel_id=1, source_target_pairs={{0,1},{1,0},{2,3},{3,2},{4,5},{5,4},{6,7},{7,6},{8,9},{9,8},{10,11... | collective-permute-start | bytes 589832 | tf_op jit(solution)/shard_map/ppermute | solution.py:112
  122.9 1.1 collective-permute-done.2
  124.0 0.9 maximum_select_fusion
  (29 shorter events, 0.8 us)
Async XLA Ops:
  0.0 43.4 %copy-start = (bf16[2048,4,128]{2,1,0:T(4,128)(2,1)S(1)}, bf16[2048,4,128]{2,1,0:T(4,128)(2,1)}, u32[]{:S(2)}) copy-start(bf16[2048,4,128]{2,1,0:T(4,128)(2,1)} %param.12) | copy-start | bytes 6291460
  5.8 9.7 %copy-start.4 = (s32[80]{0:T(128)S(1)}, s32[80]{0:T(128)}, u32[]{:S(2)}) copy-start(s32[80]{0:T(128)} %param.16) | copy-start | bytes 964
  5.8 9.9 %copy-start.3 = (s32[80]{0:T(128)S(1)}, s32[80]{0:T(128)}, u32[]{:S(2)}) copy-start(s32[80]{0:T(128)} %param.17) | copy-start | bytes 964
  7.7 29.6 %copy-start.5 = (f32[2048]{0:T(1024)S(1)}, f32[2048]{0:T(1024)}, u32[]{:S(2)}) copy-start(f32[2048]{0:T(1024)} %param.10) | copy-start | bytes 24580
  7.7 26.1 %all-to-all-start = ((bf16[16,5,64,128]{3,2,1,0:T(8,128)(2,1)}), bf16[16,5,64,128]{3,2,1,0:T(8,128)(2,1)}, u32[]{:S(2)}, u32[]{:S(2)}) async-start(bf16[16,5,64,128]{3,2,1,0:T(8,128)(2,1)} %bitcast.33), calls=%async_computation | async-start | bytes 2621440 | tf_op jit(solution)/shard_map/all_to_all | solution.py:71
  33.8 11.8 %collective-permute-start = (bf16[16,5,64,128]{3,2,1,0:T(8,128)(2,1)}, bf16[16,5,64,128]{3,2,1,0:T(8,128)(2,1)}, u32[]{:S(2)}, u32[]{:S(2)}) collective-permute-start(bf16[16,5,64,128]{3,2,1,0:T(8,128)(2,1)} %all-to-all-done), channel_id=1, source_target_pairs={{0,1},{1,0},{2,3},{3,2},{4,5},{5,4},{6,7},{7,6},{8,9},{9,8},{10,11... | collective-permute-start | bytes 3932168 | tf_op jit(solution)/shard_map/ppermute | solution.py:73
  41.9 2.7 %copy-start.2 = (bf16[768,2048]{1,0:T(8,128)(2,1)S(1)}, bf16[768,2048]{1,0:T(8,128)(2,1)}, u32[]{:S(2)}) copy-start(bf16[768,2048]{1,0:T(8,128)(2,1)} %param.9) | copy-start | bytes 9437188
  54.8 1.7 %copy-start.1 = (bf16[160,64,128]{2,1,0:T(8,128)(2,1)S(1)}, bf16[160,64,128]{2,1,0:T(8,128)(2,1)}, u32[]{:S(2)}) copy-start(bf16[160,64,128]{2,1,0:T(8,128)(2,1)} %gather_fusion.3) | copy-start | bytes 7864324
  89.7 1.8 %collective-permute-start.1 = (bf16[768,256]{1,0:T(8,128)(2,1)S(1)}, bf16[768,256]{1,0:T(8,128)(2,1)S(1)}, u32[]{:S(2)}, u32[]{:S(2)}) collective-permute-start(bf16[768,256]{1,0:T(8,128)(2,1)S(1)} %shard_map.91), channel_id=1, source_target_pairs={{0,1},{1,0},{2,3},{3,2},{4,5},{5,4},{6,7},{7,6},{8,9},{9,8},{10,11... | collective-permute-start | bytes 1179656 | tf_op jit(solution)/shard_map/ppermute | solution.py:92
  92.9 25.5 %all-to-all-start.1 = ((bf16[4,384,512]{2,1,0:T(8,128)(2,1)}), bf16[4,384,512]{2,1,0:T(8,128)(2,1)}, u32[]{:S(2)}, u32[]{:S(2)}) async-start(bf16[4,384,512]{2,1,0:T(8,128)(2,1)} %broadcast_in_dim.16), calls=%async_computation.1 | async-start | bytes 3145728 | tf_op jit(solution)/shard_map/all_to_all | solution.py:102
  121.5 2.5 %collective-permute-start.2 = (bf16[384,256]{1,0:T(8,128)(2,1)S(1)}, bf16[384,256]{1,0:T(8,128)(2,1)S(1)}, u32[]{:S(2)}, u32[]{:S(2)}) collective-permute-start(bf16[384,256]{1,0:T(8,128)(2,1)S(1)} %get-tuple-element.8), channel_id=1, source_target_pairs={{0,1},{1,0},{2,3},{3,2},{4,5},{5,4},{6,7},{7,6},{8,9},{9,8},{10,11... | collective-permute-start | bytes 589832 | tf_op jit(solution)/shard_map/ppermute | solution.py:112
